TPU v7x, 128 devices: a whole 4x4x4 slice. The times are simulated.
128 devices in a mesh: seq: 32 (over z, y, core), tp: 4 (over x).
Axes of the slice: x: 4, y: 4, z: 4, core: 2. Of those that a mesh axis runs over, the one named last changes fastest.
Arguments:
- tokens: bfloat16 [16384, 1408], P('seq'), may hold values from -70 to 70
- group_image: int32 [4096], P('seq'), may hold values from 0 to 31, never falling along the last dimension, each value on 1 to 512 neighbouring positions
- image_slot: int32 [32], replicated, may hold values from 0 to 31, each once
- attention_gain: float32 [1408], replicated, may hold values from 0.1 to 1.9
- query_weight: bfloat16 [1408, 1408], P(None, 'tp'), may hold values from -1.11930376 to 1.11930376
- key_weight: bfloat16 [1408, 1408], P(None, 'tp'), may hold values from -1.11930376 to 1.11930376
- value_weight: bfloat16 [1408, 1408], P(None, 'tp'), may hold values from -1.25 to 1.25
- output_weight: bfloat16 [1408, 1408], P('tp'), may hold values from -0.15625 to 0.15625
- feedforward_gain: float32 [1408], replicated, may hold values from 0.1 to 1.9
- up_weight: bfloat16 [1408, 6144], P(None, 'tp'), may hold values from -0.15625 to 0.15625
- down_weight: bfloat16 [6144, 1408], P('tp'), may hold values from -0.078125 to 0.078125
- merge_gain: float32 [1408], replicated, may hold values from 0.1 to 1.9
- merge_weight: bfloat16 [5632, 3584], P(None, 'tp'), may hold values from -0.078125 to 0.078125
Outputs:
- merged_rows: bfloat16 [32, 512, 3584], P('seq', None, 'tp')
Inputs may be any that keep to these rules, and one draw needn't show every extreme that they name: `group_image`: images are numbered in the order of their groups, each covers consecutive groups, 1 to 512 of them, and one covers exactly 512.
All inputs are finite; a program needn't handle non-finite values.
Results may differ from a plain program's by a relative error of at most 0.012.
Values may be sent and summed in bfloat16 or wider, within the bound.
No kernel may reach another device: no remote copies, remote signals or barrier semaphores. Data moves between devices by JAX's collectives and lax.ppermute only.
A program may use at most 192 MiB of HBM per device.

v0:
```python
import jax
import jax.numpy as jnp
from jax import lax
from jax.sharding import PartitionSpec as P

D = 1408
HD = 88
REACH = 4


epsilon = 1e-06
masked_score = -1e30


def shifted(value, axis, steps):
    count = lax.axis_size(axis)
    initial, last = (max(0, -steps), min(count, count - steps))
    return lax.ppermute(value, axis, [(source, source + steps) for source in range(initial, last)])


def finish_norm(hidden, row_mean, square, norm_gain):
    return (
        (hidden - row_mean) * lax.rsqrt(square - row_mean * row_mean + epsilon) * norm_gain
    ).astype(jnp.bfloat16)


def full_norm(hidden, norm_gain):
    row_mean = jnp.mean(hidden, axis=1, keepdims=True)
    square = jnp.mean(hidden * hidden, axis=1, keepdims=True)
    return finish_norm(hidden, row_mean, square, norm_gain)


def sum_rows(partial_value):
    return lax.psum(partial_value, "tp")


def attend_window(query_heads, key_heads, value_heads, query_image, key_image):
    scores = jnp.einsum(
        "qhd,khd->hqk", query_heads, key_heads, preferred_element_type=jnp.float32
    ) * HD ** (-0.5)
    same_image = query_image[:, None] == key_image[None, :]
    scores = jnp.where(same_image[None], scores, masked_score)
    row_best = jnp.max(scores, axis=2, keepdims=True)
    weights = jnp.exp(scores - row_best)
    row_total = jnp.sum(weights, axis=2)
    weighted = jnp.einsum(
        "hqk,khd->qhd",
        weights.astype(jnp.bfloat16),
        value_heads,
        preferred_element_type=jnp.float32,
    )
    return weighted / jnp.transpose(row_total)[:, :, None]


def shards(
    tokens,
    group_image,
    image_slot,
    attention_gain,
    query_weight,
    key_weight,
    value_weight,
    output_weight,
    feedforward_gain,
    up_weight,
    down_weight,
    merge_gain,
    merge_weight,
):
    device = lax.axis_index("seq")
    seq_count = lax.axis_size("seq")
    token_rows = tokens.shape[0]
    group_rows = group_image.shape[0]
    group_table = lax.all_gather(group_image, "seq", axis=0, tiled=True)
    token_image = jnp.repeat(group_table, 4)
    query_image = lax.dynamic_slice_in_dim(token_image, device * token_rows, token_rows, 0)
    residual = tokens.astype(jnp.float32)
    normed = full_norm(residual, attention_gain)
    head_count = query_weight.shape[1] // HD
    queries = jnp.dot(normed, query_weight, preferred_element_type=jnp.float32).astype(jnp.bfloat16)
    key_rows = jnp.dot(normed, key_weight, preferred_element_type=jnp.float32).astype(jnp.bfloat16)
    value_rows = jnp.dot(normed, value_weight, preferred_element_type=jnp.float32).astype(
        jnp.bfloat16
    )
    query_heads = queries.reshape(token_rows, head_count, HD)
    key_value = jnp.stack([key_rows, value_rows])
    arrived = []
    for offset in range(REACH, -REACH - 1, -1):
        if offset == 0:
            arrived.append(key_value)
        else:
            arrived.append(shifted(key_value, "seq", offset))
    window = jnp.concatenate(arrived, axis=1)
    reach_rows = REACH * token_rows
    image_pad = jnp.full((reach_rows,), -1, jnp.int32)
    image_padded = jnp.concatenate([image_pad, token_image, image_pad], axis=0)
    key_image = lax.dynamic_slice_in_dim(
        image_padded, device * token_rows, (2 * REACH + 1) * token_rows, 0
    )
    context = attend_window(
        query_heads,
        window[0].reshape(-1, head_count, HD),
        window[1].reshape(-1, head_count, HD),
        query_image,
        key_image,
    )
    context = context.astype(jnp.bfloat16).reshape(token_rows, head_count * HD)
    attention_part = jnp.dot(context, output_weight, preferred_element_type=jnp.float32)
    after_attention = residual + sum_rows(attention_part)
    normed_two = full_norm(after_attention, feedforward_gain)
    hidden_units = jax.nn.gelu(
        jnp.dot(normed_two, up_weight, preferred_element_type=jnp.float32), approximate=False
    ).astype(jnp.bfloat16)
    after_feedforward = after_attention + sum_rows(
        jnp.dot(hidden_units, down_weight, preferred_element_type=jnp.float32)
    )
    normed_three = full_norm(after_feedforward, merge_gain)
    grouped = normed_three.reshape(group_rows, 4 * D)
    projected = jnp.dot(grouped, merge_weight, preferred_element_type=jnp.float32).astype(
        jnp.bfloat16
    )
    image_count = image_slot.shape[0]
    image_ids = jnp.arange(image_count, dtype=jnp.int32)
    own_image = jnp.sum(jnp.where(image_slot == device, image_ids, 0))
    first_group = jnp.sum((group_table < own_image).astype(jnp.int32))
    group_count = jnp.sum((group_table == own_image).astype(jnp.int32))
    most_rows = REACH * group_rows
    row_numbers = jnp.arange(most_rows, dtype=jnp.int32)
    kept_rows = row_numbers < group_count
    out_cols = projected.shape[1]
    my_images = lax.dynamic_slice_in_dim(group_table, device * group_rows, group_rows, 0)
    target = jnp.sum(
        jnp.where(my_images[:, None] == image_ids[None, :], image_slot[None, :], 0), axis=1
    )
    owners = jnp.arange(seq_count, dtype=jnp.int32)
    outgoing = jnp.where(
        (target[None, :] == owners[:, None])[:, :, None],
        projected[None],
        jnp.zeros((), jnp.bfloat16),
    )
    received = lax.all_to_all(outgoing, "seq", split_axis=0, concat_axis=0, tiled=True).reshape(
        seq_count * group_rows, out_cols
    )
    padded = jnp.concatenate([received, jnp.zeros((most_rows, out_cols), jnp.bfloat16)], axis=0)
    own_block = lax.dynamic_slice_in_dim(padded, first_group, most_rows, 0)
    return jnp.where(kept_rows[:, None], own_block, jnp.zeros((), jnp.bfloat16))[None]


def solution(mesh):
    return jax.shard_map(
        shards,
        mesh=mesh,
        in_specs=(
            P("seq", None),
            P("seq"),
            P(),
            P(),
            P(None, "tp"),
            P(None, "tp"),
            P(None, "tp"),
            P("tp", None),
            P(),
            P(None, "tp"),
            P("tp", None),
            P(),
            P(None, "tp"),
        ),
        out_specs=P("seq", None, "tp"),
        check_vma=False,
    )
```

profile of v0, /device:TPU:1, one launch (start us, length us, event | category | flops | bytes accessed | tf_op | source)
XLA Modules:
  0.0 493.8 jit_solution(5010891190266689677)
XLA Ops:
  6.5 0.0 copy-start
  6.5 0.0 all-reduce.4.cloned.1.call-start
  6.5 2.0 convert_reduce_fusion
  8.6 1.9 fusion.18
  10.5 0.0 copy-start.10
  10.5 0.8 fusion.63
  11.2 1.0 copy-done.10
  12.2 0.8 fusion.62
  13.0 1.0 pad_maximum_fusion
  13.9 3.3 collective-permute-start.4
  17.3 3.2 collective-permute-start.3
  20.5 4.1 collective-permute-start.2
  24.6 4.0 collective-permute-start.1
  28.6 4.4 collective-permute-start
  33.0 62.8 %all-gather = s32[32,1,128]{2,1,0:T(1,128)S(1)} all-gather(s32[1,1,128]{2,1,0:T(1,128)S(1)} %bitcast.42), channel_id=1, replica_groups=mesh['seq'=32,'tp'=4] {'seq'}, dimensions={0}, use_global_device_ids=true | all-gather | bytes 16896 | tf_op jit(solution)/shard_map/all_gather | solution.py:74
  95.8 0.6 broadcast_in_dim.97
  96.4 1.6 reshape.126
  98.0 0.1 dynamic_slice.13
  98.1 0.1 fusion.73
  98.2 1.3 broadcast_compare_fusion
  99.6 3.2 convolution_convert_fusion
  102.7 0.0 collective-permute-done
  102.7 1.4 collective-permute-start.5
  104.1 1.2 constant_dynamic-update-slice_fusion.8
  105.3 0.0 collective-permute-done.1
  105.3 1.3 collective-permute-start.6
  106.6 1.2 constant_dynamic-update-slice_fusion.7
  107.8 0.0 collective-permute-done.2
  107.8 1.5 collective-permute-start.7
  109.3 1.2 constant_dynamic-update-slice_fusion.6
  110.4 0.0 collective-permute-done.3
  110.4 1.2 constant_dynamic-update-slice_fusion.5
  111.7 0.0 collective-permute-done.4
  111.7 1.2 constant_dynamic-update-slice_fusion.3
  112.8 9.7 %collective-permute-done.5 = bf16[2,512,352]{1,2,0:T(8,128)(2,1)S(1)} collective-permute-done((bf16[2,512,352]{1,2,0:T(8,128)(2,1)}, bf16[2,512,352]{1,2,0:T(8,128)(2,1)S(1)}, u32[]{:S(2)}, u32[]{:S(2)}) %collective-permute-start.5) | collective-permute-done | bytes 720928 | tf_op jit(solution)/shard_map/ppermute | solution.py:18
  122.6 1.0 collective-permute-done.6
  123.6 7.9 %collective-permute-done.7 = bf16[2,512,352]{1,2,0:T(8,128)(2,1)S(1)} collective-permute-done((bf16[2,512,352]{1,2,0:T(8,128)(2,1)}, bf16[2,512,352]{1,2,0:T(8,128)(2,1)S(1)}, u32[]{:S(2)}, u32[]{:S(2)}) %collective-permute-start.7) | collective-permute-done | bytes 720928 | tf_op jit(solution)/shard_map/ppermute | solution.py:18
  131.5 3.1 fusion.109
  134.7 18.3 %fusion = (f32[4,512]{1,0:T(4,128)S(1)}, f32[4,512,4608]{2,1,0:T(8,128)}) fusion(pred[512,4608]{1,0:T(8,128)(4,1)S(1)} %broadcast_compare_fusion, bf16[512,4,88]{0,2,1:T(8,128)(2,1)S(1)} %bitcast.43, bf16[4608,4,88]{0,2,1:T(8,128)(2,1)} %bitcast.36), kind=kOutput, calls=%fused_computation.2 | convolution fusion | flops 1689253888 | bytes 43720704 | tf_op jit(solution)/shard_map/qhd,khd->hqk/dot_general | solution.py:38
  153.0 17.5 %fusion.1 = f32[4,512]{1,0:T(4,128)S(1)} fusion(f32[4,512,4608]{2,1,0:T(8,128)} %get-tuple-element.23, f32[4,512]{1,0:T(4,128)S(1)} %get-tuple-element.22, pred[512,4608]{1,0:T(8,128)(4,1)S(1)} %broadcast_compare_fusion), kind=kLoop, calls=%fused_computation.3 | loop fusion | flops 37746688 | bytes 40124416 | tf_op jit(solution)/shard_map/reduce_sum | solution.py:45
  170.4 15.3 %fusion.67 = bf16[512,4,88]{0,2,1:T(8,128)(2,1)S(1)} fusion(bf16[4608,4,88]{0,2,1:T(8,128)(2,1)S(1)} %bitcast.35, f32[4,512,4608]{2,1,0:T(8,128)} %get-tuple-element.23, f32[4,512]{1,0:T(4,128)S(1)} %get-tuple-element.22, pred[512,4608]{1,0:T(8,128)(4,1)S(1)} %broadcast_compare_fusion, f32[512,4]{0,1:T(4,128)S(1)} %bitcast.41), kind=kOutput, calls=%fused_computation.84 | convolution fusion | flops 1699053568 | bytes 43728896 | tf_op jit(solution)/shard_map/hqk,khd->qhd/dot_general | solution.py:46
  185.7 0.0 copy-start.2
  185.7 2.6 fusion.110
  188.4 0.0 all-reduce.4.cloned.1.call-update
  188.4 0.3 all-reduce.6.cloned.1.call-start
  188.6 93.9 %all-reduce.4.cloned.1.call-done = f32[512,1408]{1,0:T(8,128)} async-done(((f32[512,1408]{1,0:T(8,128)}), f32[512,1408]{1,0:T(8,128)}) %all-reduce.4.cloned.1.call-update) | async-done | bytes 2883600 | tf_op jit(solution)/shard_map/psum | solution.py:34
  282.6 2.5 fusion.71
  285.0 0.0 copy-start.12
  285.1 16.2 %fusion.20 = f32[512,1408]{1,0:T(8,128)} fusion(bf16[1536,1408]{1,0:T(8,128)(2,1)} %param.23, bf16[1408,1536]{1,0:T(8,128)(2,1)} %param.22, f32[1408]{0:T(1024)S(1)} %copy-done.11, f32[512]{0:T(512)S(1)} %get-tuple-element.19, f32[512]{0:T(512)S(1)} %get-tuple-element.18, f32[512,1408]{1,0:T(8,128)} %all-reduce.4.cloned.1.call-done, ...), kind=kOutput, calls=%fused_computation.41 | convolution fusion | flops 4484628480 | bytes 15869440 | tf_op jit(solution)/shard_map/dot_general | solution.py:115
  301.3 0.0 all-reduce.6.cloned.1.call-update
  301.3 0.1 dynamic_slice.12
  301.4 0.1 select_reduce_fusion
  301.5 71.2 %all-reduce.6.cloned.1.call-done = f32[512,1408]{1,0:T(8,128)} async-done(((f32[512,1408]{1,0:T(8,128)}), f32[512,1408]{1,0:T(8,128)}) %all-reduce.6.cloned.1.call-update) | async-done | bytes 2883600 | tf_op jit(solution)/shard_map/psum | solution.py:34
  372.8 3.4 fusion.107
  376.2 1.6 multiply_convert_fusion
  377.8 2.7 reshape.129
  380.4 5.5 %convolution_convert_fusion.3 = bf16[128,896]{1,0:T(8,128)(2,1)S(1)} fusion(bf16[128,5632]{1,0:T(8,128)(2,1)S(1)} %reshape.129, bf16[5632,896]{1,0:T(8,128)(2,1)} %param.25), kind=kOutput, calls=%fused_computation.82 | convolution fusion | flops 1291960320 | bytes 11763712 | tf_op jit(solution)/shard_map/dot_general | solution.py:119
  386.0 3.8 broadcast_select_fusion
  389.8 7.7 %all-to-all-start = ((bf16[32,128,896]{2,1,0:T(8,128)(2,1)}), bf16[32,128,896]{2,1,0:T(8,128)(2,1)}, u32[]{:S(2)}, u32[]{:S(2)}) async-start(bf16[32,128,896]{2,1,0:T(8,128)(2,1)} %broadcast_select_fusion), calls=%async_computation | async-start | bytes 14680064 | tf_op jit(solution)/shard_map/all_to_all | solution.py:141
  397.6 0.6 fusion.74
  398.2 1.4 convert_reduce_fusion.2
  401.6 0.6 iota_compare_fusion.2
  402.3 82.1 %all-to-all-done = bf16[32,128,896]{2,1,0:T(8,128)(2,1)} async-done(((bf16[32,128,896]{2,1,0:T(8,128)(2,1)}), bf16[32,128,896]{2,1,0:T(8,128)(2,1)}, u32[]{:S(2)}, u32[]{:S(2)}) %all-to-all-start) | async-done | bytes 7340064 | tf_op jit(solution)/shard_map/all_to_all | solution.py:141
  484.4 2.6 select_bitcast_fusion
  (32 shorter events, 0.3 us)
Async XLA Ops:
  6.5 179.2 %copy-start = (bf16[352,1408]{1,0:T(8,128)(2,1)S(1)}, bf16[352,1408]{1,0:T(8,128)(2,1)}, u32[]{:S(2)}) copy-start(bf16[352,1408]{1,0:T(8,128)(2,1)} %param.20) | copy-start | bytes 2973700
  6.5 3.9 copy-start.9
  6.5 276.0 %all-reduce.4.cloned.1.call-start = ((), (), s32[]{:S(2)}) async-start(), calls=%async_computation.1 | async-start | bytes 5767168 | tf_op jit(solution)/shard_map/psum | solution.py:34
  10.5 2.5 copy-start.4
  10.5 1.7 copy-start.10
  12.2 20.8 %copy-start.8 = (s32[128]{0:T(128)S(1)}, s32[128]{0:T(128)}, u32[]{:S(2)}) copy-start(s32[128]{0:T(128)} %param.14) | copy-start | bytes 1540
  13.0 1.0 copy-start.5
  13.9 97.7 %collective-permute-start.4 = (bf16[2,512,352]{1,2,0:T(8,128)(2,1)}, bf16[2,512,352]{1,2,0:T(8,128)(2,1)}, u32[]{:S(2)}, u32[]{:S(2)}) collective-permute-start(bf16[2,512,352]{1,2,0:T(8,128)(2,1)} %pad_maximum_fusion), channel_id=1, source_target_pairs={{4,0},{8,4},{12,8},{16,12},{20,16},{24,20},{28,24},{32,28},{36,32}... | collective-permute-start | bytes 2162696 | tf_op jit(solution)/shard_map/ppermute | solution.py:18
  17.3 93.1 %collective-permute-start.3 = (bf16[2,512,352]{1,2,0:T(8,128)(2,1)}, bf16[2,512,352]{1,2,0:T(8,128)(2,1)}, u32[]{:S(2)}, u32[]{:S(2)}) collective-permute-start(bf16[2,512,352]{1,2,0:T(8,128)(2,1)} %pad_maximum_fusion), channel_id=1, source_target_pairs={{0,4},{4,8},{8,12},{12,16},{16,20},{20,24},{24,28},{28,32},{32,36}... | collective-permute-start | bytes 2162696 | tf_op jit(solution)/shard_map/ppermute | solution.py:18
  20.5 87.3 %collective-permute-start.2 = (bf16[2,512,352]{1,2,0:T(8,128)(2,1)}, bf16[2,512,352]{1,2,0:T(8,128)(2,1)}, u32[]{:S(2)}, u32[]{:S(2)}) collective-permute-start(bf16[2,512,352]{1,2,0:T(8,128)(2,1)} %pad_maximum_fusion), channel_id=1, source_target_pairs={{0,8},{4,12},{8,16},{12,20},{16,24},{20,28},{24,32},{28,36},{32,40... | collective-permute-start | bytes 2162696 | tf_op jit(solution)/shard_map/ppermute | solution.py:18
  24.6 80.7 %collective-permute-start.1 = (bf16[2,512,352]{1,2,0:T(8,128)(2,1)}, bf16[2,512,352]{1,2,0:T(8,128)(2,1)}, u32[]{:S(2)}, u32[]{:S(2)}) collective-permute-start(bf16[2,512,352]{1,2,0:T(8,128)(2,1)} %pad_maximum_fusion), channel_id=1, source_target_pairs={{0,12},{4,16},{8,20},{12,24},{16,28},{20,32},{24,36},{28,40},{32,4... | collective-permute-start | bytes 2162696 | tf_op jit(solution)/shard_map/ppermute | solution.py:18
  28.6 74.1 %collective-permute-start = (bf16[2,512,352]{1,2,0:T(8,128)(2,1)}, bf16[2,512,352]{1,2,0:T(8,128)(2,1)}, u32[]{:S(2)}, u32[]{:S(2)}) collective-permute-start(bf16[2,512,352]{1,2,0:T(8,128)(2,1)} %pad_maximum_fusion), channel_id=1, source_target_pairs={{0,16},{4,20},{8,24},{12,28},{16,32},{20,36},{24,40},{28,44},{32,4... | collective-permute-start | bytes 2162696 | tf_op jit(solution)/shard_map/ppermute | solution.py:18
  102.7 8.9 %copy-start.6 = (bf16[1,512,352]{1,2,0:T(8,128)(2,1)S(1)}, bf16[1,512,352]{1,2,0:T(8,128)(2,1)}, u32[]{:S(2)}) copy-start(bf16[1,512,352]{1,2,0:T(8,128)(2,1)} %copy-done.5) | copy-start | bytes 1081348
  102.7 19.8 %collective-permute-start.5 = (bf16[2,512,352]{1,2,0:T(8,128)(2,1)}, bf16[2,512,352]{1,2,0:T(8,128)(2,1)S(1)}, u32[]{:S(2)}, u32[]{:S(2)}) collective-permute-start(bf16[2,512,352]{1,2,0:T(8,128)(2,1)} %pad_maximum_fusion), channel_id=1, source_target_pairs={{8,0},{12,4},{16,8},{20,12},{24,16},{28,20},{32,24},{36,28},{40,32... | collective-permute-start | bytes 2162696 | tf_op jit(solution)/shard_map/ppermute | solution.py:18
  105.3 18.2 %collective-permute-start.6 = (bf16[2,512,352]{1,2,0:T(8,128)(2,1)}, bf16[2,512,352]{1,2,0:T(8,128)(2,1)S(1)}, u32[]{:S(2)}, u32[]{:S(2)}) collective-permute-start(bf16[2,512,352]{1,2,0:T(8,128)(2,1)} %pad_maximum_fusion), channel_id=1, source_target_pairs={{12,0},{16,4},{20,8},{24,12},{28,16},{32,20},{36,24},{40,28},{44,3... | collective-permute-start | bytes 2162696 | tf_op jit(solution)/shard_map/ppermute | solution.py:18
  107.8 23.7 %collective-permute-start.7 = (bf16[2,512,352]{1,2,0:T(8,128)(2,1)}, bf16[2,512,352]{1,2,0:T(8,128)(2,1)S(1)}, u32[]{:S(2)}, u32[]{:S(2)}) collective-permute-start(bf16[2,512,352]{1,2,0:T(8,128)(2,1)} %pad_maximum_fusion), channel_id=1, source_target_pairs={{16,0},{20,4},{24,8},{28,12},{32,16},{36,20},{40,24},{44,28},{48,3... | collective-permute-start | bytes 2162696 | tf_op jit(solution)/shard_map/ppermute | solution.py:18
  131.5 3.2 copy-start.13
  153.0 17.5 %copy-start.3 = (bf16[1,4608,352]{1,2,0:T(8,128)(2,1)S(1)}, bf16[1,4608,352]{1,2,0:T(8,128)(2,1)}, u32[]{:S(2)}) copy-start(bf16[1,4608,352]{1,2,0:T(8,128)(2,1)} %get-tuple-element.15) | copy-start | bytes 9732100
  185.7 96.8 %copy-start.2 = (bf16[512,1408]{1,0:T(8,128)(2,1)S(1)}, bf16[512,1408]{1,0:T(8,128)(2,1)}, u32[]{:S(2)}) copy-start(bf16[512,1408]{1,0:T(8,128)(2,1)} %param.13) | copy-start | bytes 4325380
  188.3 96.7 %copy-start.11 = (f32[1408]{0:T(1024)S(1)}, f32[1408]{0:T(1024)}, u32[]{:S(2)}) copy-start(f32[1408]{0:T(1024)} %param.21) | copy-start | bytes 16900
  188.4 184.4 %all-reduce.6.cloned.1.call-start = ((), (), s32[]{:S(2)}) async-start(), calls=%async_computation.2 | async-start | bytes 5767168 | tf_op jit(solution)/shard_map/psum | solution.py:34
  285.0 16.4 %copy-start.12 = (s32[32]{0:T(128)S(1)}, s32[32]{0:T(128)}, u32[]{:S(2)}) copy-start(s32[32]{0:T(128)} %param.15) | copy-start | bytes 388
  301.5 74.7 %copy-start.7 = (f32[1408]{0:T(1024)S(1)}, f32[1408]{0:T(1024)}, u32[]{:S(2)}) copy-start(f32[1408]{0:T(1024)} %param.24) | copy-start | bytes 16900
  389.8 94.6 %all-to-all-start = ((bf16[32,128,896]{2,1,0:T(8,128)(2,1)}), bf16[32,128,896]{2,1,0:T(8,128)(2,1)}, u32[]{:S(2)}, u32[]{:S(2)}) async-start(bf16[32,128,896]{2,1,0:T(8,128)(2,1)} %broadcast_select_fusion), calls=%async_computation | async-start | bytes 14680064 | tf_op jit(solution)/shard_map/all_to_all | solution.py:141
  484.4 2.6 copy-start.1
Sparse Core Ops, SparseCore 0:
  188.5 94.0 all-reduce.3
  301.4 71.2 all-reduce.5
where the time goes:
time: 499 us; the launch traced here: 494 us
  waiting for transfers between devices  266 us (53%)
  blocking collectives  62.8 us (13%)
  matrix products  62.6 us (13%)
  other arithmetic  40.4 us (8%)
  starting transfers between devices  31.2 us (6%)
  between operations  15.8 us (3%)
  local copies, waits for them, and re-layouts  15.2 us (3%)
    psum x2, waiting for transfers between devices, sum_rows(): return lax.psum(partial_value, 'tp')  165 us
    all_to_all x1, waiting for transfers between devices, shards(): lax.all_to_all(outgoing, 'seq', split_axis=0, concat_axis=0, tiled=True)  82.1 us
    all_gather x1, blocking collectives, shards(): group_table = lax.all_gather(group_image, 'seq', axis=0, tiled=True)  62.8 us
    ppermute x8, starting transfers between devices, shifted(): lax.ppermute(value, axis, [(source, source + steps) for source in range(i...  23.2 us
    ppermute x8, waiting for transfers between devices, shifted(): lax.ppermute(value, axis, [(source, source + steps) for source in range(i...  18.5 us
    dot_general x1, matrix products, attend_window(): jnp.einsum('qhd,khd->hqk', query_heads, key_heads, preferred_element_type...  18.3 us
    reduce_sum x1, other arithmetic, attend_window(): row_total = jnp.sum(weights, axis=2)  17.5 us
    dot_general x1, matrix products, shards(): jnp.dot(hidden_units, down_weight, preferred_element_type=jnp.float32)  16.2 us
  transfers between devices with their start and end apart: 11, of which 6 were waited for; matrix products, arithmetic and copies ran while one was open for 3% of the time, Pallas kernels for 0%

commit v1 on v0

--- a/solution.py
+++ b/solution.py
@@ -52,6 +52,44 @@
     return weighted / jnp.transpose(row_total)[:, :, None]
 
 
+def image_of_groups(groups, starts, group_total):
+    inside = (groups >= 0) & (groups < group_total)
+    image = jnp.sum((starts[None, :] <= groups[:, None]).astype(jnp.int32), axis=1) - 1
+    return jnp.where(inside, image, -1)
+
+
+def route_to_owners(projected, starts, counts, image_slot, device, seq_count):
+    group_rows, out_cols = projected.shape
+    per_pair = group_rows // seq_count
+    spread = projected.reshape(per_pair, seq_count, out_cols).transpose(1, 0, 2)
+    spread = lax.all_to_all(spread, "seq", split_axis=0, concat_axis=0, tiled=True)
+    held = spread.reshape(group_rows, out_cols)
+    image_count = image_slot.shape[0]
+    most_rows = REACH * group_rows
+    per_owner = most_rows // seq_count
+    image_ids = jnp.arange(image_count, dtype=jnp.int32)
+    owners = jnp.arange(seq_count, dtype=jnp.int32)
+    owned_image = jnp.sum(
+        jnp.where(image_slot[None, :] == owners[:, None], image_ids[None, :], 0), axis=1
+    )
+    owner_start = starts[owned_image]
+    owner_count = counts[owned_image]
+    first_pos = jnp.mod(device - owner_start, seq_count)
+    first_row = (owner_start + first_pos - device) // seq_count
+    steps = jnp.arange(per_owner, dtype=jnp.int32)
+    rows = first_row[:, None] + steps[None, :]
+    valid = (first_pos[:, None] + seq_count * steps[None, :]) < owner_count[:, None]
+    rows = jnp.clip(rows, 0, group_rows - 1)
+    outgoing = jnp.take(held, rows.reshape(-1), axis=0).reshape(seq_count, per_owner, out_cols)
+    outgoing = jnp.where(valid[:, :, None], outgoing, jnp.zeros((), outgoing.dtype))
+    received = lax.all_to_all(outgoing, "seq", split_axis=0, concat_axis=0, tiled=True)
+    own_image = jnp.sum(jnp.where(image_slot == device, image_ids, 0))
+    own_start = starts[own_image]
+    order = jnp.mod(own_start + jnp.arange(seq_count, dtype=jnp.int32), seq_count)
+    placed = jnp.take(received, order, axis=0).transpose(1, 0, 2)
+    return placed.reshape(most_rows, out_cols)
+
+
 def shards(
     tokens,
     group_image,
@@ -71,9 +109,15 @@
     seq_count = lax.axis_size("seq")
     token_rows = tokens.shape[0]
     group_rows = group_image.shape[0]
-    group_table = lax.all_gather(group_image, "seq", axis=0, tiled=True)
-    token_image = jnp.repeat(group_table, 4)
-    query_image = lax.dynamic_slice_in_dim(token_image, device * token_rows, token_rows, 0)
+    group_total = group_rows * seq_count
+    image_count = image_slot.shape[0]
+    image_ids = jnp.arange(image_count, dtype=jnp.int32)
+    local_counts = jnp.sum(
+        (group_image[:, None] == image_ids[None, :]).astype(jnp.int32), axis=0
+    )
+    counts = lax.psum(local_counts, "seq")
+    starts = jnp.cumsum(counts) - counts
+    query_image = jnp.repeat(group_image, 4)
     residual = tokens.astype(jnp.float32)
     normed = full_norm(residual, attention_gain)
     head_count = query_weight.shape[1] // HD
@@ -91,12 +135,10 @@
         else:
             arrived.append(shifted(key_value, "seq", offset))
     window = jnp.concatenate(arrived, axis=1)
-    reach_rows = REACH * token_rows
-    image_pad = jnp.full((reach_rows,), -1, jnp.int32)
-    image_padded = jnp.concatenate([image_pad, token_image, image_pad], axis=0)
-    key_image = lax.dynamic_slice_in_dim(
-        image_padded, device * token_rows, (2 * REACH + 1) * token_rows, 0
+    window_groups = (device - REACH) * group_rows + jnp.arange(
+        (2 * REACH + 1) * group_rows, dtype=jnp.int32
     )
+    key_image = jnp.repeat(image_of_groups(window_groups, starts, group_total), 4)
     context = attend_window(
         query_heads,
         window[0].reshape(-1, head_count, HD),
@@ -119,31 +161,7 @@
     projected = jnp.dot(grouped, merge_weight, preferred_element_type=jnp.float32).astype(
         jnp.bfloat16
     )
-    image_count = image_slot.shape[0]
-    image_ids = jnp.arange(image_count, dtype=jnp.int32)
-    own_image = jnp.sum(jnp.where(image_slot == device, image_ids, 0))
-    first_group = jnp.sum((group_table < own_image).astype(jnp.int32))
-    group_count = jnp.sum((group_table == own_image).astype(jnp.int32))
-    most_rows = REACH * group_rows
-    row_numbers = jnp.arange(most_rows, dtype=jnp.int32)
-    kept_rows = row_numbers < group_count
-    out_cols = projected.shape[1]
-    my_images = lax.dynamic_slice_in_dim(group_table, device * group_rows, group_rows, 0)
-    target = jnp.sum(
-        jnp.where(my_images[:, None] == image_ids[None, :], image_slot[None, :], 0), axis=1
-    )
-    owners = jnp.arange(seq_count, dtype=jnp.int32)
-    outgoing = jnp.where(
-        (target[None, :] == owners[:, None])[:, :, None],
-        projected[None],
-        jnp.zeros((), jnp.bfloat16),
-    )
-    received = lax.all_to_all(outgoing, "seq", split_axis=0, concat_axis=0, tiled=True).reshape(
-        seq_count * group_rows, out_cols
-    )
-    padded = jnp.concatenate([received, jnp.zeros((most_rows, out_cols), jnp.bfloat16)], axis=0)
-    own_block = lax.dynamic_slice_in_dim(padded, first_group, most_rows, 0)
-    return jnp.where(kept_rows[:, None], own_block, jnp.zeros((), jnp.bfloat16))[None]
+    return route_to_owners(projected, starts, counts, image_slot, device, seq_count)[None]
 
 
 def solution(mesh):

time: 499 us -> 420 us (0.84)
  waiting for transfers between devices: 266 us -> 203 us
  blocking collectives: 62.8 us -> 47.7 us
  local copies, waits for them, and re-layouts: 15.2 us -> 20.4 us
  other arithmetic: 40.4 us -> 35.2 us
    all_gather x1 -> x0, blocking collectives: 62.8 us -> none  [shards(): group_table = lax.all_gather(group_image, 'seq', axis=0, tiled=True)]
    all_to_all x1 -> x2, waiting for transfers between devices: 82.1 us -> 19.5 us  [the longest x1 11 us: route_to_owners(): lax.all_to_all(outgoing, 'seq', split_axis=0, concat_axis=0, tiled=True)]
    psum x0 -> x1, blocking collectives: none -> 47.7 us  [shards(): counts = lax.psum(local_counts, 'seq')]
    all_to_all x1 -> x2, starting transfers between devices: 7.75 us -> 11.5 us  [the longest x1 7.7 us: route_to_owners(): lax.all_to_all(spread, 'seq', split_axis=0, concat_axis=0, tiled=True)]
  transfers between devices with their start and end apart: 11 -> 12, of which waited for: 6 -> 7; matrix products, arithmetic and copies ran while one was open for 3% -> 4% of each run, Pallas kernels for 0% -> 0%
where the time goes in v1:
time: 420 us; the launch traced here: 419 us
  waiting for transfers between devices  203 us (48%)
  matrix products  61.8 us (15%)
  blocking collectives  47.7 us (11%)
  other arithmetic  35.2 us (8%)
  starting transfers between devices  35 us (8%)
  local copies, waits for them, and re-layouts  20.4 us (5%)
  between operations  16 us (4%)
    psum x2, waiting for transfers between devices, sum_rows(): return lax.psum(partial_value, 'tp')  163 us
    psum x1, blocking collectives, shards(): counts = lax.psum(local_counts, 'seq')  47.7 us
    ppermute x8, starting transfers between devices, shifted(): lax.ppermute(value, axis, [(source, source + steps) for source in range(i...  23.2 us
    ppermute x8, waiting for transfers between devices, shifted(): lax.ppermute(value, axis, [(source, source + steps) for source in range(i...  19.6 us
    dot_general x1, matrix products, attend_window(): jnp.einsum('qhd,khd->hqk', query_heads, key_heads, preferred_element_type...  18.3 us
    reduce_sum x1, other arithmetic, attend_window(): row_total = jnp.sum(weights, axis=2)  17.4 us
    dot_general x1, matrix products, shards(): jnp.dot(hidden_units, down_weight, preferred_element_type=jnp.float32)  16.2 us
    dot_general x1, matrix products, attend_window(): jnp.einsum('hqk,khd->qhd', weights.astype(jnp.bfloat16), value_heads, pre...  15.3 us
  transfers between devices with their start and end apart: 12, of which 7 were waited for; matrix products, arithmetic and copies ran while one was open for 4% of the time, Pallas kernels for 0%

profile of v1, /device:TPU:1, one launch (start us, length us, event | category | flops | bytes accessed | tf_op | source)
XLA Modules:
  0.0 418.6 jit_solution(13911761281440724261)
XLA Ops:
  6.5 2.0 convert_reduce_fusion
  8.6 1.9 fusion.18
  10.5 0.8 fusion.63
  11.2 1.0 copy-done.12
  12.2 0.8 fusion.62
  13.0 1.0 pad_maximum_fusion
  13.9 6.5 %collective-permute-start = (bf16[2,512,352]{1,2,0:T(8,128)(2,1)}, bf16[2,512,352]{1,2,0:T(8,128)(2,1)}, u32[]{:S(2)}, u32[]{:S(2)}) collective-permute-start(bf16[2,512,352]{1,2,0:T(8,128)(2,1)} %pad_maximum_fusion), channel_id=1, source_target_pairs={{0,16},{4,20},{8,24},{12,28},{16,32},{20,36},{24,40},{28,44},{32,4... | collective-permute-start | bytes 2162696 | tf_op jit(solution)/shard_map/ppermute | solution.py:18
  20.5 4.1 collective-permute-start.1
  24.6 3.2 collective-permute-start.2
  27.9 1.9 collective-permute-start.3
  29.8 3.2 collective-permute-start.4
  33.1 0.1 convert_reduce_fusion.2
  33.2 47.7 %psum.21 = s32[32]{0:T(128)S(1)} all-reduce(s32[32]{0:T(128)S(1)} %convert_reduce_fusion.2), channel_id=1, replica_groups=mesh['seq'=32,'tp'=4] {'seq'}, use_global_device_ids=true, to_apply=%region_1.0 | all-reduce | flops 32 | bytes 256 | tf_op jit(solution)/shard_map/psum | solution.py:118
  80.9 0.1 copy.23
  81.0 0.1 reduce
  81.1 0.1 convert_reduce_fusion.1
  81.3 0.2 broadcast_in_dim.103
  81.5 0.3 eq.66
  81.9 0.1 eq.64
  82.0 1.3 broadcast_compare_fusion
  83.3 2.4 convolution_convert_fusion
  85.8 1.4 collective-permute-start.5
  87.2 1.2 constant_dynamic-update-slice_fusion.8
  88.4 1.3 collective-permute-start.6
  89.7 1.2 constant_dynamic-update-slice_fusion.7
  90.8 1.5 collective-permute-start.7
  92.3 1.2 constant_dynamic-update-slice_fusion.6
  93.5 1.2 constant_dynamic-update-slice_fusion.5
  94.7 1.2 constant_dynamic-update-slice_fusion.3
  95.9 7.1 %collective-permute-done.5 = bf16[2,512,352]{1,2,0:T(8,128)(2,1)S(1)} collective-permute-done((bf16[2,512,352]{1,2,0:T(8,128)(2,1)}, bf16[2,512,352]{1,2,0:T(8,128)(2,1)S(1)}, u32[]{:S(2)}, u32[]{:S(2)}) %collective-permute-start.5) | collective-permute-done | bytes 720928 | tf_op jit(solution)/shard_map/ppermute | solution.py:18
  103.0 2.5 collective-permute-done.6
  105.5 10.1 %collective-permute-done.7 = bf16[2,512,352]{1,2,0:T(8,128)(2,1)S(1)} collective-permute-done((bf16[2,512,352]{1,2,0:T(8,128)(2,1)}, bf16[2,512,352]{1,2,0:T(8,128)(2,1)S(1)}, u32[]{:S(2)}, u32[]{:S(2)}) %collective-permute-start.7) | collective-permute-done | bytes 720928 | tf_op jit(solution)/shard_map/ppermute | solution.py:18
  115.7 3.1 fusion.112
  118.8 18.3 %fusion = (f32[4,512]{1,0:T(4,128)S(1)}, f32[4,512,4608]{2,1,0:T(8,128)}) fusion(pred[512,4608]{1,0:T(8,128)(4,1)S(1)} %broadcast_compare_fusion, bf16[512,4,88]{0,2,1:T(8,128)(2,1)S(1)} %bitcast.55, bf16[4608,4,88]{0,2,1:T(8,128)(2,1)} %bitcast.50), kind=kOutput, calls=%fused_computation.6 | convolution fusion | flops 1689253888 | bytes 43720704 | tf_op jit(solution)/shard_map/qhd,khd->hqk/dot_general | solution.py:38
  137.1 17.4 %fusion.1 = f32[4,512]{1,0:T(4,128)S(1)} fusion(f32[4,512,4608]{2,1,0:T(8,128)} %get-tuple-element.23, f32[4,512]{1,0:T(4,128)S(1)} %get-tuple-element.22, pred[512,4608]{1,0:T(8,128)(4,1)S(1)} %broadcast_compare_fusion), kind=kLoop, calls=%fused_computation.7 | loop fusion | flops 37746688 | bytes 40124416 | tf_op jit(solution)/shard_map/reduce_sum | solution.py:45
  154.6 15.3 %fusion.67 = bf16[512,4,88]{0,2,1:T(8,128)(2,1)S(1)} fusion(bf16[4608,4,88]{0,2,1:T(8,128)(2,1)S(1)} %bitcast.49, f32[4,512,4608]{2,1,0:T(8,128)} %get-tuple-element.23, f32[4,512]{1,0:T(4,128)S(1)} %get-tuple-element.22, pred[512,4608]{1,0:T(8,128)(4,1)S(1)} %broadcast_compare_fusion, f32[512,4]{0,1:T(4,128)S(1)} %bitcast.53), kind=kOutput, calls=%fused_computation.86 | convolution fusion | flops 1699053568 | bytes 43728896 | tf_op jit(solution)/shard_map/hqk,khd->qhd/dot_general | solution.py:46
  169.9 2.6 fusion.113
  172.5 0.3 all-reduce.5.cloned.1.call-start
  172.8 93.7 %all-reduce.3.cloned.1.call-done = f32[512,1408]{1,0:T(8,128)} async-done(((f32[512,1408]{1,0:T(8,128)}), f32[512,1408]{1,0:T(8,128)}) %all-reduce.3.cloned.1.call-update) | async-done | bytes 2883600 | tf_op jit(solution)/shard_map/psum | solution.py:34
  266.5 2.4 fusion.71
  268.9 16.2 %fusion.20 = f32[512,1408]{1,0:T(8,128)} fusion(bf16[1536,1408]{1,0:T(8,128)(2,1)} %param.23, bf16[1408,1536]{1,0:T(8,128)(2,1)} %param.22, f32[1408]{0:T(1024)S(1)} %copy-done.13, f32[512]{0:T(512)S(1)} %get-tuple-element.19, f32[512]{0:T(512)S(1)} %get-tuple-element.18, f32[512,1408]{1,0:T(8,128)} %all-reduce.3.cloned.1.call-done, ...), kind=kOutput, calls=%fused_computation.43 | convolution fusion | flops 4484628480 | bytes 15869440 | tf_op jit(solution)/shard_map/dot_general | solution.py:157
  285.1 0.1 select_reduce_fusion
  285.3 0.7 gather_fusion
  286.0 0.7 gather_fusion.1
  286.8 0.1 min.12
  286.9 69.7 %all-reduce.5.cloned.1.call-done = f32[512,1408]{1,0:T(8,128)} async-done(((f32[512,1408]{1,0:T(8,128)}), f32[512,1408]{1,0:T(8,128)}) %all-reduce.5.cloned.1.call-update) | async-done | bytes 2883600 | tf_op jit(solution)/shard_map/psum | solution.py:34
  356.6 3.3 fusion.110
  359.9 1.6 multiply_convert_fusion
  361.5 2.7 reshape.342
  364.2 5.6 %convolution_convert_fusion.3 = bf16[128,896]{1,0:T(8,128)(2,1)S(1)} fusion(bf16[128,5632]{1,0:T(8,128)(2,1)S(1)} %reshape.342, bf16[5632,896]{1,0:T(8,128)(2,1)} %param.25), kind=kOutput, calls=%fused_computation.84 | convolution fusion | flops 1291960320 | bytes 11763712 | tf_op jit(solution)/shard_map/dot_general | solution.py:161
  369.7 0.8 copy.27
  370.6 7.7 %all-to-all-start = ((bf16[32,4,896]{2,1,0:T(4,128)(2,1)}), bf16[32,4,896]{2,1,0:T(4,128)(2,1)S(1)}, u32[]{:S(2)}, u32[]{:S(2)}) async-start(bf16[32,4,896]{2,1,0:T(4,128)(2,1)} %bitcast.46), calls=%async_computation | async-start | bytes 458752 | tf_op jit(solution)/shard_map/all_to_all | solution.py:65
  378.4 8.5 %all-to-all-done = bf16[32,4,896]{2,1,0:T(4,128)(2,1)S(1)} async-done(((bf16[32,4,896]{2,1,0:T(4,128)(2,1)}), bf16[32,4,896]{2,1,0:T(4,128)(2,1)S(1)}, u32[]{:S(2)}, u32[]{:S(2)}) %all-to-all-start) | async-done | bytes 229408 | tf_op jit(solution)/shard_map/all_to_all | solution.py:65
  386.9 2.1 gather_fusion.2
  389.0 1.2 select_select_fusion
  390.2 3.8 all-to-all-start.1
  394.0 0.7 fusion.72
  396.7 0.7 dynamic_slice.3
  397.4 0.7 fusion.77
  398.1 0.7 compare_and_fusion.1
  398.8 11.0 %all-to-all-done.1 = bf16[32,16,896]{2,1,0:T(8,128)(2,1)S(1)} async-done(((bf16[32,16,896]{2,1,0:T(8,128)(2,1)}), bf16[32,16,896]{2,1,0:T(8,128)(2,1)S(1)}, u32[]{:S(2)}, u32[]{:S(2)}) %all-to-all-start.1) | async-done | bytes 917536 | tf_op jit(solution)/shard_map/all_to_all | solution.py:85
  409.8 0.7 gather_fusion.3
  410.5 0.2 select_bitcast_fusion
  410.7 1.1 copy.25
  (59 shorter events, 0.8 us)
Async XLA Ops:
  6.5 163.3 %copy-start = (bf16[352,1408]{1,0:T(8,128)(2,1)S(1)}, bf16[352,1408]{1,0:T(8,128)(2,1)}, u32[]{:S(2)}) copy-start(bf16[352,1408]{1,0:T(8,128)(2,1)} %param.20) | copy-start | bytes 2973700
  6.5 3.9 copy-start.11
  6.5 259.9 %all-reduce.3.cloned.1.call-start = ((), (), s32[]{:S(2)}) async-start(), calls=%async_computation.2 | async-start | bytes 5767168 | tf_op jit(solution)/shard_map/psum | solution.py:34
  10.5 2.5 copy-start.4
  10.5 1.7 copy-start.12
  12.2 1.8 copy-start.5
  12.2 20.9 %copy-start.10 = (s32[128]{0:T(128)S(1)}, s32[128]{0:T(128)}, u32[]{:S(2)}) copy-start(s32[128]{0:T(128)} %param.14) | copy-start | bytes 1540
  13.0 7.5 %copy-start.7 = (bf16[1,512,352]{1,2,0:T(8,128)(2,1)}, bf16[1,512,352]{1,2,0:T(8,128)(2,1)S(1)}, u32[]{:S(2)}) copy-start(bf16[1,512,352]{1,2,0:T(8,128)(2,1)S(1)} %fusion.62) | copy-start | bytes 1081348
  13.9 71.8 %collective-permute-start = (bf16[2,512,352]{1,2,0:T(8,128)(2,1)}, bf16[2,512,352]{1,2,0:T(8,128)(2,1)}, u32[]{:S(2)}, u32[]{:S(2)}) collective-permute-start(bf16[2,512,352]{1,2,0:T(8,128)(2,1)} %pad_maximum_fusion), channel_id=1, source_target_pairs={{0,16},{4,20},{8,24},{12,28},{16,32},{20,36},{24,40},{28,44},{32,4... | collective-permute-start | bytes 2162696 | tf_op jit(solution)/shard_map/ppermute | solution.py:18
  20.5 67.9 %collective-permute-start.1 = (bf16[2,512,352]{1,2,0:T(8,128)(2,1)}, bf16[2,512,352]{1,2,0:T(8,128)(2,1)}, u32[]{:S(2)}, u32[]{:S(2)}) collective-permute-start(bf16[2,512,352]{1,2,0:T(8,128)(2,1)} %pad_maximum_fusion), channel_id=1, source_target_pairs={{0,12},{4,16},{8,20},{12,24},{16,28},{20,32},{24,36},{28,40},{32,4... | collective-permute-start | bytes 2162696 | tf_op jit(solution)/shard_map/ppermute | solution.py:18
  24.6 66.2 %collective-permute-start.2 = (bf16[2,512,352]{1,2,0:T(8,128)(2,1)}, bf16[2,512,352]{1,2,0:T(8,128)(2,1)}, u32[]{:S(2)}, u32[]{:S(2)}) collective-permute-start(bf16[2,512,352]{1,2,0:T(8,128)(2,1)} %pad_maximum_fusion), channel_id=1, source_target_pairs={{0,8},{4,12},{8,16},{12,20},{16,24},{20,28},{24,32},{28,36},{32,40... | collective-permute-start | bytes 2162696 | tf_op jit(solution)/shard_map/ppermute | solution.py:18
  27.9 65.6 %collective-permute-start.3 = (bf16[2,512,352]{1,2,0:T(8,128)(2,1)}, bf16[2,512,352]{1,2,0:T(8,128)(2,1)}, u32[]{:S(2)}, u32[]{:S(2)}) collective-permute-start(bf16[2,512,352]{1,2,0:T(8,128)(2,1)} %pad_maximum_fusion), channel_id=1, source_target_pairs={{0,4},{4,8},{8,12},{12,16},{16,20},{20,24},{24,28},{28,32},{32,36}... | collective-permute-start | bytes 2162696 | tf_op jit(solution)/shard_map/ppermute | solution.py:18
  29.8 65.0 %collective-permute-start.4 = (bf16[2,512,352]{1,2,0:T(8,128)(2,1)}, bf16[2,512,352]{1,2,0:T(8,128)(2,1)}, u32[]{:S(2)}, u32[]{:S(2)}) collective-permute-start(bf16[2,512,352]{1,2,0:T(8,128)(2,1)} %pad_maximum_fusion), channel_id=1, source_target_pairs={{4,0},{8,4},{12,8},{16,12},{20,16},{24,20},{28,24},{32,28},{36,32}... | collective-permute-start | bytes 2162696 | tf_op jit(solution)/shard_map/ppermute | solution.py:18
  85.7 8.9 %copy-start.6 = (bf16[1,512,352]{1,2,0:T(8,128)(2,1)S(1)}, bf16[1,512,352]{1,2,0:T(8,128)(2,1)}, u32[]{:S(2)}) copy-start(bf16[1,512,352]{1,2,0:T(8,128)(2,1)} %copy-done.5) | copy-start | bytes 1081348
  85.7 8.9 %copy-start.8 = (bf16[1,512,352]{1,2,0:T(8,128)(2,1)S(1)}, bf16[1,512,352]{1,2,0:T(8,128)(2,1)}, u32[]{:S(2)}) copy-start(bf16[1,512,352]{1,2,0:T(8,128)(2,1)} %copy-done.7) | copy-start | bytes 1081348
  85.8 17.2 %collective-permute-start.5 = (bf16[2,512,352]{1,2,0:T(8,128)(2,1)}, bf16[2,512,352]{1,2,0:T(8,128)(2,1)S(1)}, u32[]{:S(2)}, u32[]{:S(2)}) collective-permute-start(bf16[2,512,352]{1,2,0:T(8,128)(2,1)} %pad_maximum_fusion), channel_id=1, source_target_pairs={{8,0},{12,4},{16,8},{20,12},{24,16},{28,20},{32,24},{36,28},{40,32... | collective-permute-start | bytes 2162696 | tf_op jit(solution)/shard_map/ppermute | solution.py:18
  88.4 17.1 %collective-permute-start.6 = (bf16[2,512,352]{1,2,0:T(8,128)(2,1)}, bf16[2,512,352]{1,2,0:T(8,128)(2,1)S(1)}, u32[]{:S(2)}, u32[]{:S(2)}) collective-permute-start(bf16[2,512,352]{1,2,0:T(8,128)(2,1)} %pad_maximum_fusion), channel_id=1, source_target_pairs={{12,0},{16,4},{20,8},{24,12},{28,16},{32,20},{36,24},{40,28},{44,3... | collective-permute-start | bytes 2162696 | tf_op jit(solution)/shard_map/ppermute | solution.py:18
  90.8 24.8 %collective-permute-start.7 = (bf16[2,512,352]{1,2,0:T(8,128)(2,1)}, bf16[2,512,352]{1,2,0:T(8,128)(2,1)S(1)}, u32[]{:S(2)}, u32[]{:S(2)}) collective-permute-start(bf16[2,512,352]{1,2,0:T(8,128)(2,1)} %pad_maximum_fusion), channel_id=1, source_target_pairs={{16,0},{20,4},{24,8},{28,12},{32,16},{36,20},{40,24},{44,28},{48,3... | collective-permute-start | bytes 2162696 | tf_op jit(solution)/shard_map/ppermute | solution.py:18
  137.1 17.5 %copy-start.3 = (bf16[1,4608,352]{1,2,0:T(8,128)(2,1)S(1)}, bf16[1,4608,352]{1,2,0:T(8,128)(2,1)}, u32[]{:S(2)}) copy-start(bf16[1,4608,352]{1,2,0:T(8,128)(2,1)} %get-tuple-element.15) | copy-start | bytes 9732100
  169.8 96.6 %copy-start.2 = (bf16[512,1408]{1,0:T(8,128)(2,1)S(1)}, bf16[512,1408]{1,0:T(8,128)(2,1)}, u32[]{:S(2)}) copy-start(bf16[512,1408]{1,0:T(8,128)(2,1)} %param.13) | copy-start | bytes 4325380
  172.5 96.4 %copy-start.13 = (f32[1408]{0:T(1024)S(1)}, f32[1408]{0:T(1024)}, u32[]{:S(2)}) copy-start(f32[1408]{0:T(1024)} %param.21) | copy-start | bytes 16900
  172.5 184.1 %all-reduce.5.cloned.1.call-start = ((), (), s32[]{:S(2)}) async-start(), calls=%async_computation.3 | async-start | bytes 5767168 | tf_op jit(solution)/shard_map/psum | solution.py:34
  268.9 16.2 %copy-start.14 = (s32[32]{0:T(128)S(1)}, s32[32]{0:T(128)}, u32[]{:S(2)}) copy-start(s32[32]{0:T(128)} %param.15) | copy-start | bytes 388
  286.9 73.0 %copy-start.9 = (f32[1408]{0:T(1024)S(1)}, f32[1408]{0:T(1024)}, u32[]{:S(2)}) copy-start(f32[1408]{0:T(1024)} %param.24) | copy-start | bytes 16900
  370.6 16.3 %all-to-all-start = ((bf16[32,4,896]{2,1,0:T(4,128)(2,1)}), bf16[32,4,896]{2,1,0:T(4,128)(2,1)S(1)}, u32[]{:S(2)}, u32[]{:S(2)}) async-start(bf16[32,4,896]{2,1,0:T(4,128)(2,1)} %bitcast.46), calls=%async_computation | async-start | bytes 458752 | tf_op jit(solution)/shard_map/all_to_all | solution.py:65
  390.2 19.7 %all-to-all-start.1 = ((bf16[32,16,896]{2,1,0:T(8,128)(2,1)}), bf16[32,16,896]{2,1,0:T(8,128)(2,1)S(1)}, u32[]{:S(2)}, u32[]{:S(2)}) async-start(bf16[32,16,896]{2,1,0:T(8,128)(2,1)} %select_select_fusion), calls=%async_computation.1 | async-start | bytes 1835008 | tf_op jit(solution)/shard_map/all_to_all | solution.py:85
  393.9 17.8 %copy-start.1 = (bf16[352,1408]{1,0:T(8,128)(2,1)S(1)}, bf16[352,1408]{1,0:T(8,128)(2,1)}, u32[]{:S(2)}) copy-start(bf16[352,1408]{1,0:T(8,128)(2,1)} %param.20) | copy-start | bytes 2973700
Sparse Core Ops, SparseCore 0:
  172.6 93.8 all-reduce.2
  285.3 71.2 all-reduce.4

commit v2 on v1

--- a/solution.py
+++ b/solution.py
@@ -31,7 +31,15 @@
 
 
 def sum_rows(partial_value):
-    return lax.psum(partial_value, "tp")
+    tp_count = lax.axis_size("tp")
+    rows, cols = partial_value.shape
+    pieces = partial_value.astype(jnp.bfloat16).reshape(tp_count, rows // tp_count, cols)
+    pieces = lax.all_to_all(pieces, "tp", split_axis=0, concat_axis=0, tiled=True)
+    return jnp.sum(pieces.astype(jnp.float32), axis=0)
+
+
+def gather_rows(row_block):
+    return lax.all_gather(row_block, "tp", axis=0, tiled=True)
 
 
 def attend_window(query_heads, key_heads, value_heads, query_image, key_image):
@@ -115,7 +123,14 @@
     local_counts = jnp.sum(
         (group_image[:, None] == image_ids[None, :]).astype(jnp.int32), axis=0
     )
-    counts = lax.psum(local_counts, "seq")
+    every_count = lax.all_to_all(
+        jnp.broadcast_to(local_counts[None, :], (seq_count, image_count)),
+        "seq",
+        split_axis=0,
+        concat_axis=0,
+        tiled=True,
+    )
+    counts = jnp.sum(every_count, axis=0)
     starts = jnp.cumsum(counts) - counts
     query_image = jnp.repeat(group_image, 4)
     residual = tokens.astype(jnp.float32)
@@ -148,15 +163,18 @@
     )
     context = context.astype(jnp.bfloat16).reshape(token_rows, head_count * HD)
     attention_part = jnp.dot(context, output_weight, preferred_element_type=jnp.float32)
-    after_attention = residual + sum_rows(attention_part)
-    normed_two = full_norm(after_attention, feedforward_gain)
+    tp_count = lax.axis_size("tp")
+    own_rows = token_rows // tp_count
+    own_residual = lax.dynamic_slice_in_dim(residual, lax.axis_index("tp") * own_rows, own_rows, 0)
+    after_attention = own_residual + sum_rows(attention_part)
+    normed_two = gather_rows(full_norm(after_attention, feedforward_gain))
     hidden_units = jax.nn.gelu(
         jnp.dot(normed_two, up_weight, preferred_element_type=jnp.float32), approximate=False
     ).astype(jnp.bfloat16)
     after_feedforward = after_attention + sum_rows(
         jnp.dot(hidden_units, down_weight, preferred_element_type=jnp.float32)
     )
-    normed_three = full_norm(after_feedforward, merge_gain)
+    normed_three = gather_rows(full_norm(after_feedforward, merge_gain))
     grouped = normed_three.reshape(group_rows, 4 * D)
     projected = jnp.dot(grouped, merge_weight, preferred_element_type=jnp.float32).astype(
         jnp.bfloat16

time: 420 us -> 360 us (0.86)
  waiting for transfers between devices: 203 us -> 162 us
  blocking collectives: 47.7 us -> 20.4 us
  starting transfers between devices: 35 us -> 46.1 us
    psum x2 -> x0, waiting for transfers between devices: 163 us -> none  [sum_rows(): return lax.psum(partial_value, 'tp')]
    all_gather x0 -> x2, waiting for transfers between devices: none -> 73.6 us  [gather_rows(): return lax.all_gather(row_block, 'tp', axis=0, tiled=True)]
    all_to_all x0 -> x2, waiting for transfers between devices: none -> 49.8 us  [the longest x1 36.8 us: shards(): lax.all_to_all(jnp.broadcast_to(local_counts[None, :], (seq_count, image_...]
    psum x1 -> x0, blocking collectives: 47.7 us -> none  [shards(): counts = lax.psum(local_counts, 'seq')]
    all_to_all x0 -> x1, blocking collectives: none -> 20.4 us  [sum_rows(): lax.all_to_all(pieces, 'tp', split_axis=0, concat_axis=0, tiled=True)]
    all_to_all x0 -> x2, starting transfers between devices: none -> 10.9 us  [the longest x1 6.58 us: shards(): lax.all_to_all(jnp.broadcast_to(local_counts[None, :], (seq_count, image_...]
  transfers between devices with their start and end apart: 12 -> 14, of which waited for: 7 -> 9; matrix products, arithmetic and copies ran while one was open for 4% -> 5% of each run, Pallas kernels for 0% -> 0%
where the time goes in v2:
time: 360 us; the launch traced here: 358 us
  waiting for transfers between devices  162 us (45%)
  matrix products  58.7 us (16%)
  starting transfers between devices  46.1 us (13%)
  other arithmetic  34.9 us (10%)
  local copies, waits for them, and re-layouts  20.5 us (6%)
  blocking collectives  20.4 us (6%)
  between operations  16 us (4%)
    all_gather x2, waiting for transfers between devices, gather_rows(): return lax.all_gather(row_block, 'tp', axis=0, tiled=True)  73.6 us
    all_to_all x1, waiting for transfers between devices, shards(): lax.all_to_all(jnp.broadcast_to(local_counts[None, :], (seq_count, image_...  36.8 us
    ppermute x8, starting transfers between devices, shifted(): lax.ppermute(value, axis, [(source, source + steps) for source in range(i...  23.1 us
    all_to_all x1, blocking collectives, sum_rows(): lax.all_to_all(pieces, 'tp', split_axis=0, concat_axis=0, tiled=True)  20.4 us
    ppermute x8, waiting for transfers between devices, shifted(): lax.ppermute(value, axis, [(source, source + steps) for source in range(i...  19 us
    dot_general x1, matrix products, attend_window(): jnp.einsum('qhd,khd->hqk', query_heads, key_heads, preferred_element_type...  18.3 us
    reduce_sum x1, other arithmetic, attend_window(): row_total = jnp.sum(weights, axis=2)  17.5 us
    dot_general x1, matrix products, attend_window(): jnp.einsum('hqk,khd->qhd', weights.astype(jnp.bfloat16), value_heads, pre...  15.3 us
  transfers between devices with their start and end apart: 14, of which 9 were waited for; matrix products, arithmetic and copies ran while one was open for 5% of the time, Pallas kernels for 0%

profile of v2, /device:TPU:1, one launch (start us, length us, event | category | flops | bytes accessed | tf_op | source)
XLA Modules:
  0.0 358.4 jit_solution(18022457232259990420)
XLA Ops:
  6.5 2.0 convert_reduce_fusion.2
  8.6 1.9 multiply_convert_fusion
  10.5 0.8 fusion.51
  11.2 0.4 copy-done.8
  11.7 0.8 fusion.50
  12.4 0.9 pad_maximum_fusion
  13.3 6.5 %collective-permute-start = (bf16[2,512,352]{1,2,0:T(8,128)(2,1)}, bf16[2,512,352]{1,2,0:T(8,128)(2,1)}, u32[]{:S(2)}, u32[]{:S(2)}) collective-permute-start(bf16[2,512,352]{1,2,0:T(8,128)(2,1)} %pad_maximum_fusion), channel_id=1, source_target_pairs={{0,16},{4,20},{8,24},{12,28},{16,32},{20,36},{24,40},{28,44},{32,4... | collective-permute-start | bytes 2162696 | tf_op jit(solution)/shard_map/ppermute | solution.py:18
  19.8 4.2 %collective-permute-start.1 = (bf16[2,512,352]{1,2,0:T(8,128)(2,1)}, bf16[2,512,352]{1,2,0:T(8,128)(2,1)}, u32[]{:S(2)}, u32[]{:S(2)}) collective-permute-start(bf16[2,512,352]{1,2,0:T(8,128)(2,1)} %pad_maximum_fusion), channel_id=1, source_target_pairs={{0,12},{4,16},{8,20},{12,24},{16,28},{20,32},{24,36},{28,40},{32,4... | collective-permute-start | bytes 2162696 | tf_op jit(solution)/shard_map/ppermute | solution.py:18
  24.0 3.2 collective-permute-start.2
  27.3 1.9 collective-permute-start.3
  29.2 3.3 collective-permute-start.4
  32.6 0.6 broadcast_in_dim.60
  33.2 6.6 %all-to-all-start = ((s32[32,1,32]{2,1,0:T(1,128)}), s32[32,1,32]{2,1,0:T(1,128)S(1)}, u32[]{:S(2)}, u32[]{:S(2)}) async-start(s32[32,1,32]{2,1,0:T(1,128)} %broadcast_in_dim.60), calls=%async_computation | async-start | bytes 32768 | tf_op jit(solution)/shard_map/all_to_all | solution.py:126
  39.8 2.0 convolution_convert_fusion.2
  42.0 36.8 %all-to-all-done = s32[32,1,32]{2,1,0:T(1,128)S(1)} async-done(((s32[32,1,32]{2,1,0:T(1,128)}), s32[32,1,32]{2,1,0:T(1,128)S(1)}, u32[]{:S(2)}, u32[]{:S(2)}) %all-to-all-start) | async-done | bytes 4128 | tf_op jit(solution)/shard_map/all_to_all | solution.py:126
  79.2 0.2 broadcast_in_dim.110
  79.4 0.3 eq.66
  79.7 1.3 broadcast_compare_fusion
  81.1 1.3 collective-permute-start.5
  82.4 1.2 constant_dynamic-update-slice_fusion.8
  83.6 1.3 collective-permute-start.6
  84.9 1.2 constant_dynamic-update-slice_fusion.7
  86.0 1.5 collective-permute-start.7
  87.5 1.2 constant_dynamic-update-slice_fusion.6
  88.7 1.2 constant_dynamic-update-slice_fusion.5
  89.9 1.2 constant_dynamic-update-slice_fusion.3
  91.1 9.2 %collective-permute-done.5 = bf16[2,512,352]{1,2,0:T(8,128)(2,1)S(1)} collective-permute-done((bf16[2,512,352]{1,2,0:T(8,128)(2,1)}, bf16[2,512,352]{1,2,0:T(8,128)(2,1)S(1)}, u32[]{:S(2)}, u32[]{:S(2)}) %collective-permute-start.5) | collective-permute-done | bytes 720928 | tf_op jit(solution)/shard_map/ppermute | solution.py:18
  100.3 2.0 collective-permute-done.6
  102.3 7.9 %collective-permute-done.7 = bf16[2,512,352]{1,2,0:T(8,128)(2,1)S(1)} collective-permute-done((bf16[2,512,352]{1,2,0:T(8,128)(2,1)}, bf16[2,512,352]{1,2,0:T(8,128)(2,1)S(1)}, u32[]{:S(2)}, u32[]{:S(2)}) %collective-permute-start.7) | collective-permute-done | bytes 720928 | tf_op jit(solution)/shard_map/ppermute | solution.py:18
  110.3 3.1 fusion.98
  113.4 18.3 %fusion = (f32[4,512]{1,0:T(4,128)S(1)}, f32[4,512,4608]{2,1,0:T(8,128)}) fusion(pred[512,4608]{1,0:T(8,128)(4,1)S(1)} %broadcast_compare_fusion, bf16[512,4,88]{0,2,1:T(8,128)(2,1)S(1)} %bitcast.62, bf16[4608,4,88]{0,2,1:T(8,128)(2,1)} %bitcast.55), kind=kOutput, calls=%fused_computation.6 | convolution fusion | flops 1689253888 | bytes 43720704 | tf_op jit(solution)/shard_map/qhd,khd->hqk/dot_general | solution.py:46
  131.7 17.5 %fusion.1 = f32[4,512]{1,0:T(4,128)S(1)} fusion(f32[4,512,4608]{2,1,0:T(8,128)} %get-tuple-element.24, f32[4,512]{1,0:T(4,128)S(1)} %get-tuple-element.23, pred[512,4608]{1,0:T(8,128)(4,1)S(1)} %broadcast_compare_fusion), kind=kLoop, calls=%fused_computation.7 | loop fusion | flops 37746688 | bytes 40124416 | tf_op jit(solution)/shard_map/reduce_sum | solution.py:53
  149.2 15.3 %fusion.55 = bf16[512,4,88]{0,2,1:T(8,128)(2,1)S(1)} fusion(bf16[4608,4,88]{0,2,1:T(8,128)(2,1)S(1)} %bitcast.54, f32[4,512,4608]{2,1,0:T(8,128)} %get-tuple-element.24, f32[4,512]{1,0:T(4,128)S(1)} %get-tuple-element.23, pred[512,4608]{1,0:T(8,128)(4,1)S(1)} %broadcast_compare_fusion, f32[512,4]{0,1:T(4,128)S(1)} %bitcast.60), kind=kOutput, calls=%fused_computation.76 | convolution fusion | flops 1699053568 | bytes 43728896 | tf_op jit(solution)/shard_map/hqk,khd->qhd/dot_general | solution.py:54
  164.5 2.1 convolution_convert_fusion.1
  166.6 4.3 %all-to-all-start.1 = ((bf16[4,128,1408]{2,1,0:T(8,128)(2,1)}), bf16[4,128,1408]{2,1,0:T(8,128)(2,1)}, u32[]{:S(2)}, u32[]{:S(2)}) async-start(bf16[4,128,1408]{2,1,0:T(8,128)(2,1)} %bitcast.52), calls=%async_computation.1 | async-start | bytes 2883584 | tf_op jit(solution)/shard_map/all_to_all | solution.py:37
  171.0 1.8 convert_element_type.52
  172.8 13.0 %all-to-all-done.1 = bf16[4,128,1408]{2,1,0:T(8,128)(2,1)} async-done(((bf16[4,128,1408]{2,1,0:T(8,128)(2,1)}), bf16[4,128,1408]{2,1,0:T(8,128)(2,1)}, u32[]{:S(2)}, u32[]{:S(2)}) %all-to-all-start.1) | async-done | bytes 1441824 | tf_op jit(solution)/shard_map/all_to_all | solution.py:37
  185.8 1.7 convert_reduce_fusion.1
  187.4 1.3 fusion.97
  188.8 0.9 multiply_convert_fusion.2
  189.7 0.3 all-gather.5.cloned.1.call-start
  190.0 48.7 %all-gather.3.cloned.1.call-done = bf16[512,1408]{1,0:T(8,128)(2,1)} async-done(((bf16[128,1408]{1,0:T(8,128)(2,1)}), bf16[512,1408]{1,0:T(8,128)(2,1)}) %all-gather.3.cloned.1.call-update) | async-done | bytes 1441808 | tf_op jit(solution)/shard_map/all_gather | solution.py:42
  238.7 14.0 %convolution_convert_fusion = bf16[512,1408]{1,0:T(8,128)(2,1)S(1)} fusion(bf16[1536,1408]{1,0:T(8,128)(2,1)} %param.23, bf16[512,1408]{1,0:T(8,128)(2,1)} %all-gather.3.cloned.1.call-done, bf16[1408,1536]{1,0:T(8,128)(2,1)} %param.22), kind=kOutput, calls=%fused_computation.31 | convolution fusion | flops 4481024000 | bytes 11534336 | tf_op jit(solution)/shard_map/dot_general | solution.py:175
  252.7 20.4 %all_to_all.26 = bf16[4,128,1408]{2,1,0:T(8,128)(2,1)S(1)} all-to-all(bf16[4,128,1408]{2,1,0:T(8,128)(2,1)S(1)} %bitcast.56), channel_id=1, replica_groups=mesh['seq'=32,'tp'=4] {'tp'}, dimensions={0} | all-to-all | bytes 2883584 | tf_op jit(solution)/shard_map/all_to_all | solution.py:37
  273.3 0.2 fusion.96
  273.5 0.9 multiply_convert_fusion.1
  274.6 0.7 gather_fusion
  275.3 0.7 gather_fusion.1
  276.2 24.9 %all-gather.5.cloned.1.call-done = bf16[512,1408]{1,0:T(8,128)(2,1)} async-done(((bf16[128,1408]{1,0:T(8,128)(2,1)}), bf16[512,1408]{1,0:T(8,128)(2,1)}) %all-gather.5.cloned.1.call-update) | async-done | bytes 1441808 | tf_op jit(solution)/shard_map/all_gather | solution.py:42
  301.1 2.7 reshape.352
  303.8 5.5 %convolution_convert_fusion.5 = bf16[128,896]{1,0:T(8,128)(2,1)S(1)} fusion(bf16[128,5632]{1,0:T(8,128)(2,1)S(1)} %reshape.352, bf16[5632,896]{1,0:T(8,128)(2,1)} %param.25), kind=kOutput, calls=%fused_computation.74 | convolution fusion | flops 1291960320 | bytes 11763712 | tf_op jit(solution)/shard_map/dot_general | solution.py:179
  309.3 0.8 copy.31
  310.1 7.9 %all-to-all-start.3 = ((bf16[32,4,896]{2,1,0:T(4,128)(2,1)}), bf16[32,4,896]{2,1,0:T(4,128)(2,1)S(1)}, u32[]{:S(2)}, u32[]{:S(2)}) async-start(bf16[32,4,896]{2,1,0:T(4,128)(2,1)} %bitcast.50), calls=%async_computation.3 | async-start | bytes 458752 | tf_op jit(solution)/shard_map/all_to_all | solution.py:73
  318.1 8.5 %all-to-all-done.3 = bf16[32,4,896]{2,1,0:T(4,128)(2,1)S(1)} async-done(((bf16[32,4,896]{2,1,0:T(4,128)(2,1)}), bf16[32,4,896]{2,1,0:T(4,128)(2,1)S(1)}, u32[]{:S(2)}, u32[]{:S(2)}) %all-to-all-start.3) | async-done | bytes 229408 | tf_op jit(solution)/shard_map/all_to_all | solution.py:73
  326.7 2.1 gather_fusion.2
  328.8 1.2 select_select_fusion
  329.9 3.8 %all-to-all-start.4 = ((bf16[32,16,896]{2,1,0:T(8,128)(2,1)}), bf16[32,16,896]{2,1,0:T(8,128)(2,1)S(1)}, u32[]{:S(2)}, u32[]{:S(2)}) async-start(bf16[32,16,896]{2,1,0:T(8,128)(2,1)} %select_select_fusion), calls=%async_computation.4 | async-start | bytes 1835008 | tf_op jit(solution)/shard_map/all_to_all | solution.py:93
  333.7 0.7 fusion.58
  336.5 0.7 dynamic_slice.6
  337.2 0.7 fusion.63
  337.9 0.7 compare_and_fusion.1
  338.6 11.0 %all-to-all-done.4 = bf16[32,16,896]{2,1,0:T(8,128)(2,1)S(1)} async-done(((bf16[32,16,896]{2,1,0:T(8,128)(2,1)}), bf16[32,16,896]{2,1,0:T(8,128)(2,1)S(1)}, u32[]{:S(2)}, u32[]{:S(2)}) %all-to-all-start.4) | async-done | bytes 917536 | tf_op jit(solution)/shard_map/all_to_all | solution.py:93
  349.6 0.7 gather_fusion.3
  350.5 1.1 copy.29
  (59 shorter events, 1.9 us)
Async XLA Ops:
  6.5 157.9 %copy-start = (bf16[352,1408]{1,0:T(8,128)(2,1)S(1)}, bf16[352,1408]{1,0:T(8,128)(2,1)}, u32[]{:S(2)}) copy-start(bf16[352,1408]{1,0:T(8,128)(2,1)} %param.20) | copy-start | bytes 2973700
  6.5 3.9 %copy-start.7 = (bf16[1408,352]{0,1:T(8,128)(2,1)S(1)}, bf16[1408,352]{0,1:T(8,128)(2,1)}, u32[]{:S(2)}) copy-start(bf16[1408,352]{0,1:T(8,128)(2,1)} %param.19) | copy-start | bytes 2973700
  10.5 1.2 copy-start.8
  11.7 20.8 %copy-start.6 = (s32[128]{0:T(128)S(1)}, s32[128]{0:T(128)}, u32[]{:S(2)}) copy-start(s32[128]{0:T(128)} %param.14) | copy-start | bytes 1540
  13.3 67.7 %collective-permute-start = (bf16[2,512,352]{1,2,0:T(8,128)(2,1)}, bf16[2,512,352]{1,2,0:T(8,128)(2,1)}, u32[]{:S(2)}, u32[]{:S(2)}) collective-permute-start(bf16[2,512,352]{1,2,0:T(8,128)(2,1)} %pad_maximum_fusion), channel_id=1, source_target_pairs={{0,16},{4,20},{8,24},{12,28},{16,32},{20,36},{24,40},{28,44},{32,4... | collective-permute-start | bytes 2162696 | tf_op jit(solution)/shard_map/ppermute | solution.py:18
  19.8 63.7 %collective-permute-start.1 = (bf16[2,512,352]{1,2,0:T(8,128)(2,1)}, bf16[2,512,352]{1,2,0:T(8,128)(2,1)}, u32[]{:S(2)}, u32[]{:S(2)}) collective-permute-start(bf16[2,512,352]{1,2,0:T(8,128)(2,1)} %pad_maximum_fusion), channel_id=1, source_target_pairs={{0,12},{4,16},{8,20},{12,24},{16,28},{20,32},{24,36},{28,40},{32,4... | collective-permute-start | bytes 2162696 | tf_op jit(solution)/shard_map/ppermute | solution.py:18
  24.0 62.0 %collective-permute-start.2 = (bf16[2,512,352]{1,2,0:T(8,128)(2,1)}, bf16[2,512,352]{1,2,0:T(8,128)(2,1)}, u32[]{:S(2)}, u32[]{:S(2)}) collective-permute-start(bf16[2,512,352]{1,2,0:T(8,128)(2,1)} %pad_maximum_fusion), channel_id=1, source_target_pairs={{0,8},{4,12},{8,16},{12,20},{16,24},{20,28},{24,32},{28,36},{32,40... | collective-permute-start | bytes 2162696 | tf_op jit(solution)/shard_map/ppermute | solution.py:18
  27.3 61.4 %collective-permute-start.3 = (bf16[2,512,352]{1,2,0:T(8,128)(2,1)}, bf16[2,512,352]{1,2,0:T(8,128)(2,1)}, u32[]{:S(2)}, u32[]{:S(2)}) collective-permute-start(bf16[2,512,352]{1,2,0:T(8,128)(2,1)} %pad_maximum_fusion), channel_id=1, source_target_pairs={{0,4},{4,8},{8,12},{12,16},{16,20},{20,24},{24,28},{28,32},{32,36}... | collective-permute-start | bytes 2162696 | tf_op jit(solution)/shard_map/ppermute | solution.py:18
  29.2 60.7 %collective-permute-start.4 = (bf16[2,512,352]{1,2,0:T(8,128)(2,1)}, bf16[2,512,352]{1,2,0:T(8,128)(2,1)}, u32[]{:S(2)}, u32[]{:S(2)}) collective-permute-start(bf16[2,512,352]{1,2,0:T(8,128)(2,1)} %pad_maximum_fusion), channel_id=1, source_target_pairs={{4,0},{8,4},{12,8},{16,12},{20,16},{24,20},{28,24},{32,28},{36,32}... | collective-permute-start | bytes 2162696 | tf_op jit(solution)/shard_map/ppermute | solution.py:18
  33.2 45.6 %all-to-all-start = ((s32[32,1,32]{2,1,0:T(1,128)}), s32[32,1,32]{2,1,0:T(1,128)S(1)}, u32[]{:S(2)}, u32[]{:S(2)}) async-start(s32[32,1,32]{2,1,0:T(1,128)} %broadcast_in_dim.60), calls=%async_computation | async-start | bytes 32768 | tf_op jit(solution)/shard_map/all_to_all | solution.py:126
  81.1 19.1 %collective-permute-start.5 = (bf16[2,512,352]{1,2,0:T(8,128)(2,1)}, bf16[2,512,352]{1,2,0:T(8,128)(2,1)S(1)}, u32[]{:S(2)}, u32[]{:S(2)}) collective-permute-start(bf16[2,512,352]{1,2,0:T(8,128)(2,1)} %pad_maximum_fusion), channel_id=1, source_target_pairs={{8,0},{12,4},{16,8},{20,12},{24,16},{28,20},{32,24},{36,28},{40,32... | collective-permute-start | bytes 2162696 | tf_op jit(solution)/shard_map/ppermute | solution.py:18
  83.6 18.7 %collective-permute-start.6 = (bf16[2,512,352]{1,2,0:T(8,128)(2,1)}, bf16[2,512,352]{1,2,0:T(8,128)(2,1)S(1)}, u32[]{:S(2)}, u32[]{:S(2)}) collective-permute-start(bf16[2,512,352]{1,2,0:T(8,128)(2,1)} %pad_maximum_fusion), channel_id=1, source_target_pairs={{12,0},{16,4},{20,8},{24,12},{28,16},{32,20},{36,24},{40,28},{44,3... | collective-permute-start | bytes 2162696 | tf_op jit(solution)/shard_map/ppermute | solution.py:18
  86.0 24.2 %collective-permute-start.7 = (bf16[2,512,352]{1,2,0:T(8,128)(2,1)}, bf16[2,512,352]{1,2,0:T(8,128)(2,1)S(1)}, u32[]{:S(2)}, u32[]{:S(2)}) collective-permute-start(bf16[2,512,352]{1,2,0:T(8,128)(2,1)} %pad_maximum_fusion), channel_id=1, source_target_pairs={{16,0},{20,4},{24,8},{28,12},{32,16},{36,20},{40,24},{44,28},{48,3... | collective-permute-start | bytes 2162696 | tf_op jit(solution)/shard_map/ppermute | solution.py:18
  131.7 17.5 %copy-start.3 = (bf16[1,4608,352]{1,2,0:T(8,128)(2,1)S(1)}, bf16[1,4608,352]{1,2,0:T(8,128)(2,1)}, u32[]{:S(2)}) copy-start(bf16[1,4608,352]{1,2,0:T(8,128)(2,1)} %get-tuple-element.16) | copy-start | bytes 9732100
  164.5 6.6 %copy-start.2 = (bf16[512,1408]{1,0:T(8,128)(2,1)S(1)}, bf16[512,1408]{1,0:T(8,128)(2,1)}, u32[]{:S(2)}) copy-start(bf16[512,1408]{1,0:T(8,128)(2,1)} %param.13) | copy-start | bytes 4325380
  166.6 19.1 %all-to-all-start.1 = ((bf16[4,128,1408]{2,1,0:T(8,128)(2,1)}), bf16[4,128,1408]{2,1,0:T(8,128)(2,1)}, u32[]{:S(2)}, u32[]{:S(2)}) async-start(bf16[4,128,1408]{2,1,0:T(8,128)(2,1)} %bitcast.52), calls=%async_computation.1 | async-start | bytes 2883584 | tf_op jit(solution)/shard_map/all_to_all | solution.py:37
  171.0 67.7 %all-gather.3.cloned.1.call-start = ((), (), s32[]{:S(2)}) async-start(), calls=%async_computation.5 | async-start | bytes 1802240 | tf_op jit(solution)/shard_map/all_gather | solution.py:42
  172.8 16.0 %copy-start.4 = (f32[1408]{0:T(1024)S(1)}, f32[1408]{0:T(1024)}, u32[]{:S(2)}) copy-start(f32[1408]{0:T(1024)} %param.21) | copy-start | bytes 16900
  189.7 111.4 %all-gather.5.cloned.1.call-start = ((), (), s32[]{:S(2)}) async-start(), calls=%async_computation.6 | async-start | bytes 1802240 | tf_op jit(solution)/shard_map/all_gather | solution.py:42
  252.7 20.8 %copy-start.5 = (f32[1408]{0:T(1024)S(1)}, f32[1408]{0:T(1024)}, u32[]{:S(2)}) copy-start(f32[1408]{0:T(1024)} %param.24) | copy-start | bytes 16900
  273.1 1.4 copy-start.9
  310.1 16.5 %all-to-all-start.3 = ((bf16[32,4,896]{2,1,0:T(4,128)(2,1)}), bf16[32,4,896]{2,1,0:T(4,128)(2,1)S(1)}, u32[]{:S(2)}, u32[]{:S(2)}) async-start(bf16[32,4,896]{2,1,0:T(4,128)(2,1)} %bitcast.50), calls=%async_computation.3 | async-start | bytes 458752 | tf_op jit(solution)/shard_map/all_to_all | solution.py:73
  329.9 19.7 %all-to-all-start.4 = ((bf16[32,16,896]{2,1,0:T(8,128)(2,1)}), bf16[32,16,896]{2,1,0:T(8,128)(2,1)S(1)}, u32[]{:S(2)}, u32[]{:S(2)}) async-start(bf16[32,16,896]{2,1,0:T(8,128)(2,1)} %select_select_fusion), calls=%async_computation.4 | async-start | bytes 1835008 | tf_op jit(solution)/shard_map/all_to_all | solution.py:93
  333.7 17.8 %copy-start.1 = (bf16[352,1408]{1,0:T(8,128)(2,1)S(1)}, bf16[352,1408]{1,0:T(8,128)(2,1)}, u32[]{:S(2)}) copy-start(bf16[352,1408]{1,0:T(8,128)(2,1)} %param.20) | copy-start | bytes 2973700
Sparse Core Ops, SparseCore 0:
  189.8 48.8 all-gather.2
  274.6 26.4 all-gather.4

commit v3 on v2

--- a/solution.py
+++ b/solution.py
@@ -39,7 +39,10 @@
 
 
 def gather_rows(row_block):
-    return lax.all_gather(row_block, "tp", axis=0, tiled=True)
+    tp_count = lax.axis_size("tp")
+    copies = jnp.broadcast_to(row_block[None], (tp_count,) + row_block.shape)
+    copies = lax.all_to_all(copies, "tp", split_axis=0, concat_axis=0, tiled=True)
+    return copies.reshape(tp_count * row_block.shape[0], row_block.shape[1])
 
 
 def attend_window(query_heads, key_heads, value_heads, query_image, key_image):
@@ -143,6 +146,7 @@
     )
     query_heads = queries.reshape(token_rows, head_count, HD)
     key_value = jnp.stack([key_rows, value_rows])
+    counts, key_value = lax.optimization_barrier((counts, key_value))
     arrived = []
     for offset in range(REACH, -REACH - 1, -1):
         if offset == 0:

time: 360 us -> 314 us (0.87)
  waiting for transfers between devices: 162 us -> 120 us
  between operations: 16 us -> 2.59 us
  starting transfers between devices: 46.1 us -> 56.6 us
    all_gather x2 -> x0, waiting for transfers between devices: 73.6 us -> none  [gather_rows(): return lax.all_gather(row_block, 'tp', axis=0, tiled=True)]
    all_to_all x1, waiting for transfers between devices: 36.8 us -> 0.01 us  [shards(): lax.all_to_all(jnp.broadcast_to(local_counts[None, :], (seq_count, image_...]
    ppermute x8, waiting for transfers between devices: 19 us -> 54.9 us  [shifted(): lax.ppermute(value, axis, [(source, source + steps) for source in range(i...]
    all_to_all x1 -> x2, waiting for transfers between devices: 13 us -> 32.3 us  [sum_rows(): lax.all_to_all(pieces, 'tp', split_axis=0, concat_axis=0, tiled=True)]
    all_to_all x0 -> x1, waiting for transfers between devices: none -> 13 us  [gather_rows(): lax.all_to_all(copies, 'tp', split_axis=0, concat_axis=0, tiled=True)]
    all_to_all x0 -> x1, starting transfers between devices: none -> 4.57 us  [gather_rows(): lax.all_to_all(copies, 'tp', split_axis=0, concat_axis=0, tiled=True)]
    all_to_all x1 -> x2, starting transfers between devices: 4.34 us -> 8.02 us  [sum_rows(): lax.all_to_all(pieces, 'tp', split_axis=0, concat_axis=0, tiled=True)]
  transfers between devices with their start and end apart: 14 -> 14, of which waited for: 9 -> 11; matrix products, arithmetic and copies ran while one was open for 5% -> 7% of each run, Pallas kernels for 0% -> 0%
where the time goes in v3:
time: 314 us; the launch traced here: 312 us
  waiting for transfers between devices  120 us (38%)
  matrix products  60.1 us (19%)
  starting transfers between devices  56.6 us (18%)
  other arithmetic  33.2 us (11%)
  local copies, waits for them, and re-layouts  20.7 us (7%)
  blocking collectives  19.4 us (6%)
    ppermute x8, waiting for transfers between devices, shifted(): lax.ppermute(value, axis, [(source, source + steps) for source in range(i...  54.9 us
    all_to_all x2, waiting for transfers between devices, sum_rows(): lax.all_to_all(pieces, 'tp', split_axis=0, concat_axis=0, tiled=True)  32.3 us
    ppermute x8, starting transfers between devices, shifted(): lax.ppermute(value, axis, [(source, source + steps) for source in range(i...  21.6 us
    all_to_all x1, blocking collectives, gather_rows(): lax.all_to_all(copies, 'tp', split_axis=0, concat_axis=0, tiled=True)  19.4 us
    dot_general x1, matrix products, attend_window(): jnp.einsum('qhd,khd->hqk', query_heads, key_heads, preferred_element_type...  18.3 us
    reduce_sum x1, other arithmetic, attend_window(): row_total = jnp.sum(weights, axis=2)  17.5 us
    dot_general x1, matrix products, attend_window(): jnp.einsum('hqk,khd->qhd', weights.astype(jnp.bfloat16), value_heads, pre...  15.3 us
    dot_general x1, matrix products, shards(): jnp.dot(hidden_units, down_weight, preferred_element_type=jnp.float32)  14.7 us
  transfers between devices with their start and end apart: 14, of which 11 were waited for; matrix products, arithmetic and copies ran while one was open for 7% of the time, Pallas kernels for 0%

profile of v3, /device:TPU:1, one launch (start us, length us, event | category | flops | bytes accessed | tf_op | source)
XLA Modules:
  0.0 312.3 jit_solution(5677788866352689242)
XLA Ops:
  0.0 0.9 convert_reduce_fusion.4
  0.9 0.6 broadcast_in_dim.64
  1.5 9.6 %all-to-all-start = ((s32[32,1,32]{2,1,0:T(1,128)}), s32[32,1,32]{2,1,0:T(1,128)S(1)}, u32[]{:S(2)}, u32[]{:S(2)}) async-start(s32[32,1,32]{2,1,0:T(1,128)} %broadcast_in_dim.64), calls=%async_computation | async-start | bytes 32768 | tf_op jit(solution)/shard_map/all_to_all | solution.py:129
  11.1 2.0 convert_reduce_fusion.2
  13.1 1.9 multiply_convert_fusion
  15.0 0.8 fusion.51
  15.7 0.4 copy-done.8
  16.2 0.8 fusion.50
  16.9 2.7 convolution_convert_fusion.2
  20.0 5.7 %collective-permute-start = (bf16[2,512,352]{1,2,0:T(8,128)(2,1)S(1)}, bf16[2,512,352]{1,2,0:T(8,128)(2,1)}, u32[]{:S(2)}, u32[]{:S(2)}) collective-permute-start(bf16[2,512,352]{1,2,0:T(8,128)(2,1)S(1)} %pad_maximum_fusion), channel_id=1, source_target_pairs={{0,16},{4,20},{8,24},{12,28},{16,32},{20,36},{24,40},{28,44},{32,4... | collective-permute-start | bytes 2162696 | tf_op jit(solution)/shard_map/ppermute | solution.py:18
  25.6 3.6 %collective-permute-start.1 = (bf16[2,512,352]{1,2,0:T(8,128)(2,1)S(1)}, bf16[2,512,352]{1,2,0:T(8,128)(2,1)}, u32[]{:S(2)}, u32[]{:S(2)}) collective-permute-start(bf16[2,512,352]{1,2,0:T(8,128)(2,1)S(1)} %pad_maximum_fusion), channel_id=1, source_target_pairs={{0,12},{4,16},{8,20},{12,24},{16,28},{20,32},{24,36},{28,40},{32,4... | collective-permute-start | bytes 2162696 | tf_op jit(solution)/shard_map/ppermute | solution.py:18
  29.3 3.1 collective-permute-start.2
  32.4 1.9 collective-permute-start.3
  34.3 3.3 %collective-permute-start.4 = (bf16[2,512,352]{1,2,0:T(8,128)(2,1)S(1)}, bf16[2,512,352]{1,2,0:T(8,128)(2,1)S(1)}, u32[]{:S(2)}, u32[]{:S(2)}) collective-permute-start(bf16[2,512,352]{1,2,0:T(8,128)(2,1)S(1)} %pad_maximum_fusion), channel_id=1, source_target_pairs={{4,0},{8,4},{12,8},{16,12},{20,16},{24,20},{28,24},{32,28},{36,32}... | collective-permute-start | bytes 2162696 | tf_op jit(solution)/shard_map/ppermute | solution.py:18
  38.0 0.2 broadcast_in_dim.122
  38.2 0.3 eq.66
  38.5 1.3 broadcast_compare_fusion
  40.0 1.3 collective-permute-start.5
  41.3 1.2 constant_dynamic-update-slice_fusion.8
  42.4 13.0 %collective-permute-done.1 = bf16[2,512,352]{1,2,0:T(8,128)(2,1)} collective-permute-done((bf16[2,512,352]{1,2,0:T(8,128)(2,1)S(1)}, bf16[2,512,352]{1,2,0:T(8,128)(2,1)}, u32[]{:S(2)}, u32[]{:S(2)}) %collective-permute-start.1) | collective-permute-done | bytes 720928 | tf_op jit(solution)/shard_map/ppermute | solution.py:18
  55.4 1.3 collective-permute-start.6
  56.7 1.2 constant_dynamic-update-slice_fusion.7
  57.9 13.0 %collective-permute-done.2 = bf16[2,512,352]{1,2,0:T(8,128)(2,1)} collective-permute-done((bf16[2,512,352]{1,2,0:T(8,128)(2,1)S(1)}, bf16[2,512,352]{1,2,0:T(8,128)(2,1)}, u32[]{:S(2)}, u32[]{:S(2)}) %collective-permute-start.2) | collective-permute-done | bytes 720928 | tf_op jit(solution)/shard_map/ppermute | solution.py:18
  70.9 1.5 collective-permute-start.7
  72.3 1.2 constant_dynamic-update-slice_fusion.6
  73.5 5.9 %collective-permute-done.3 = bf16[2,512,352]{1,2,0:T(8,128)(2,1)} collective-permute-done((bf16[2,512,352]{1,2,0:T(8,128)(2,1)S(1)}, bf16[2,512,352]{1,2,0:T(8,128)(2,1)}, u32[]{:S(2)}, u32[]{:S(2)}) %collective-permute-start.3) | collective-permute-done | bytes 720928 | tf_op jit(solution)/shard_map/ppermute | solution.py:18
  79.4 1.2 constant_dynamic-update-slice_fusion.5
  80.7 8.8 %collective-permute-done.6 = bf16[2,512,352]{1,2,0:T(8,128)(2,1)S(1)} collective-permute-done((bf16[2,512,352]{1,2,0:T(8,128)(2,1)S(1)}, bf16[2,512,352]{1,2,0:T(8,128)(2,1)S(1)}, u32[]{:S(2)}, u32[]{:S(2)}) %collective-permute-start.6) | collective-permute-done | bytes 720928 | tf_op jit(solution)/shard_map/ppermute | solution.py:18
  89.6 14.1 %collective-permute-done.7 = bf16[2,512,352]{1,2,0:T(8,128)(2,1)S(1)} collective-permute-done((bf16[2,512,352]{1,2,0:T(8,128)(2,1)S(1)}, bf16[2,512,352]{1,2,0:T(8,128)(2,1)S(1)}, u32[]{:S(2)}, u32[]{:S(2)}) %collective-permute-start.7) | collective-permute-done | bytes 720928 | tf_op jit(solution)/shard_map/ppermute | solution.py:18
  103.7 3.1 %fusion.98 = (bf16[1,4608,352]{1,2,0:T(8,128)(2,1)}, bf16[1,4608,352]{1,2,0:T(8,128)(2,1)}) fusion(bf16[2,4608,352]{1,2,0:T(8,128)(2,1)S(1)} %constant_dynamic-update-slice_fusion), kind=kLoop, calls=%fused_computation.175 | loop fusion | bytes 12976128 | tf_op jit(solution)/shard_map/slice | solution.py:163
  106.9 18.3 %fusion = (f32[4,512]{1,0:T(4,128)S(1)}, f32[4,512,4608]{2,1,0:T(8,128)}) fusion(pred[512,4608]{1,0:T(8,128)(4,1)S(1)} %broadcast_compare_fusion, bf16[512,4,88]{0,2,1:T(8,128)(2,1)S(1)} %bitcast.64, bf16[4608,4,88]{0,2,1:T(8,128)(2,1)} %bitcast.56), kind=kOutput, calls=%fused_computation.6 | convolution fusion | flops 1689253888 | bytes 43720704 | tf_op jit(solution)/shard_map/qhd,khd->hqk/dot_general | solution.py:49
  125.2 17.5 %fusion.1 = f32[4,512]{1,0:T(4,128)S(1)} fusion(f32[4,512,4608]{2,1,0:T(8,128)} %get-tuple-element.28, f32[4,512]{1,0:T(4,128)S(1)} %get-tuple-element.27, pred[512,4608]{1,0:T(8,128)(4,1)S(1)} %broadcast_compare_fusion), kind=kLoop, calls=%fused_computation.7 | loop fusion | flops 37746688 | bytes 40124416 | tf_op jit(solution)/shard_map/reduce_sum | solution.py:56
  142.6 15.3 %fusion.55 = bf16[512,4,88]{0,2,1:T(8,128)(2,1)S(1)} fusion(bf16[4608,4,88]{0,2,1:T(8,128)(2,1)S(1)} %bitcast.55, f32[4,512,4608]{2,1,0:T(8,128)} %get-tuple-element.28, f32[4,512]{1,0:T(4,128)S(1)} %get-tuple-element.27, pred[512,4608]{1,0:T(8,128)(4,1)S(1)} %broadcast_compare_fusion, f32[512,4]{0,1:T(4,128)S(1)} %bitcast.62), kind=kOutput, calls=%fused_computation.76 | convolution fusion | flops 1699053568 | bytes 43728896 | tf_op jit(solution)/shard_map/hqk,khd->qhd/dot_general | solution.py:57
  158.0 2.1 convolution_convert_fusion.1
  160.1 4.3 %all-to-all-start.1 = ((bf16[4,128,1408]{2,1,0:T(8,128)(2,1)}), bf16[4,128,1408]{2,1,0:T(8,128)(2,1)}, u32[]{:S(2)}, u32[]{:S(2)}) async-start(bf16[4,128,1408]{2,1,0:T(8,128)(2,1)} %bitcast.53), calls=%async_computation.1 | async-start | bytes 2883584 | tf_op jit(solution)/shard_map/all_to_all | solution.py:37
  164.5 1.8 convert_element_type.52
  166.2 16.4 %all-to-all-done.1 = bf16[4,128,1408]{2,1,0:T(8,128)(2,1)} async-done(((bf16[4,128,1408]{2,1,0:T(8,128)(2,1)}), bf16[4,128,1408]{2,1,0:T(8,128)(2,1)}, u32[]{:S(2)}, u32[]{:S(2)}) %all-to-all-start.1) | async-done | bytes 1441824 | tf_op jit(solution)/shard_map/all_to_all | solution.py:37
  182.7 1.7 convert_reduce_fusion.1
  184.3 1.3 fusion.97
  186.0 19.4 %all_to_all.36 = bf16[4,128,1408]{2,1,0:T(8,128)(2,1)S(1)} all-to-all(bf16[4,128,1408]{2,1,0:T(8,128)(2,1)S(1)} %broadcast_in_dim.125), channel_id=1, replica_groups=mesh['seq'=32,'tp'=4] {'tp'}, dimensions={0} | all-to-all | bytes 2883584 | tf_op jit(solution)/shard_map/all_to_all | solution.py:44
  205.3 14.7 %convolution_convert_fusion = bf16[512,1408]{1,0:T(8,128)(2,1)} fusion(bf16[1536,1408]{1,0:T(8,128)(2,1)} %param.23, bf16[512,1408]{1,0:T(8,128)(2,1)S(1)} %bitcast.58, bf16[1408,1536]{1,0:T(8,128)(2,1)} %param.22), kind=kOutput, calls=%fused_computation.31 | convolution fusion | flops 4481024000 | bytes 11534336 | tf_op jit(solution)/shard_map/dot_general | solution.py:179
  220.0 3.7 %all-to-all-start.3 = ((bf16[4,128,1408]{2,1,0:T(8,128)(2,1)}), bf16[4,128,1408]{2,1,0:T(8,128)(2,1)S(1)}, u32[]{:S(2)}, u32[]{:S(2)}) async-start(bf16[4,128,1408]{2,1,0:T(8,128)(2,1)} %bitcast.57), calls=%async_computation.3 | async-start | bytes 2883584 | tf_op jit(solution)/shard_map/all_to_all | solution.py:37
  223.8 15.8 %all-to-all-done.3 = bf16[4,128,1408]{2,1,0:T(8,128)(2,1)S(1)} async-done(((bf16[4,128,1408]{2,1,0:T(8,128)(2,1)}), bf16[4,128,1408]{2,1,0:T(8,128)(2,1)S(1)}, u32[]{:S(2)}, u32[]{:S(2)}) %all-to-all-start.3) | async-done | bytes 1441824 | tf_op jit(solution)/shard_map/all_to_all | solution.py:37
  239.9 0.2 fusion.96
  240.3 1.2 broadcast_in_dim.126
  241.5 4.6 %all-to-all-start.4 = ((bf16[4,128,1408]{2,1,0:T(8,128)(2,1)}), bf16[4,128,1408]{2,1,0:T(8,128)(2,1)}, u32[]{:S(2)}, u32[]{:S(2)}) async-start(bf16[4,128,1408]{2,1,0:T(8,128)(2,1)} %broadcast_in_dim.126), calls=%async_computation.4 | async-start | bytes 2883584 | tf_op jit(solution)/shard_map/all_to_all | solution.py:44
  246.1 0.7 gather_fusion
  247.0 0.7 gather_fusion.1
  247.7 13.0 %all-to-all-done.4 = bf16[4,128,1408]{2,1,0:T(8,128)(2,1)} async-done(((bf16[4,128,1408]{2,1,0:T(8,128)(2,1)}), bf16[4,128,1408]{2,1,0:T(8,128)(2,1)}, u32[]{:S(2)}, u32[]{:S(2)}) %all-to-all-start.4) | async-done | bytes 1441824 | tf_op jit(solution)/shard_map/all_to_all | solution.py:44
  260.7 2.7 reshape_reshape.3
  263.3 5.5 %convolution_convert_fusion.5 = bf16[128,896]{1,0:T(8,128)(2,1)S(1)} fusion(bf16[128,5632]{1,0:T(8,128)(2,1)S(1)} %reshape_reshape.3, bf16[5632,896]{1,0:T(8,128)(2,1)} %param.25), kind=kOutput, calls=%fused_computation.74 | convolution fusion | flops 1291960320 | bytes 11763712 | tf_op jit(solution)/shard_map/dot_general | solution.py:183
  268.9 0.8 copy.31
  269.7 9.0 %all-to-all-start.5 = ((bf16[32,4,896]{2,1,0:T(4,128)(2,1)}), bf16[32,4,896]{2,1,0:T(4,128)(2,1)S(1)}, u32[]{:S(2)}, u32[]{:S(2)}) async-start(bf16[32,4,896]{2,1,0:T(4,128)(2,1)} %bitcast.51), calls=%async_computation.5 | async-start | bytes 458752 | tf_op jit(solution)/shard_map/all_to_all | solution.py:76
  278.8 8.6 %all-to-all-done.5 = bf16[32,4,896]{2,1,0:T(4,128)(2,1)S(1)} async-done(((bf16[32,4,896]{2,1,0:T(4,128)(2,1)}), bf16[32,4,896]{2,1,0:T(4,128)(2,1)S(1)}, u32[]{:S(2)}, u32[]{:S(2)}) %all-to-all-start.5) | async-done | bytes 229408 | tf_op jit(solution)/shard_map/all_to_all | solution.py:76
  287.4 2.1 gather_fusion.2
  289.5 1.2 select_select_fusion
  290.7 3.8 %all-to-all-start.6 = ((bf16[32,16,896]{2,1,0:T(8,128)(2,1)}), bf16[32,16,896]{2,1,0:T(8,128)(2,1)S(1)}, u32[]{:S(2)}, u32[]{:S(2)}) async-start(bf16[32,16,896]{2,1,0:T(8,128)(2,1)} %select_select_fusion), calls=%async_computation.6 | async-start | bytes 1835008 | tf_op jit(solution)/shard_map/all_to_all | solution.py:96
  294.5 0.7 fusion.58
  297.3 0.7 dynamic_slice.6
  297.9 0.7 fusion.63
  298.6 0.7 compare_and_fusion.1
  299.4 11.0 %all-to-all-done.6 = bf16[32,16,896]{2,1,0:T(8,128)(2,1)S(1)} async-done(((bf16[32,16,896]{2,1,0:T(8,128)(2,1)}), bf16[32,16,896]{2,1,0:T(8,128)(2,1)S(1)}, u32[]{:S(2)}, u32[]{:S(2)}) %all-to-all-start.6) | async-done | bytes 917536 | tf_op jit(solution)/shard_map/all_to_all | solution.py:96
  310.3 0.7 gather_fusion.3
  311.2 1.1 copy.29
  (61 shorter events, 2.4 us)
Async XLA Ops:
  0.0 158.0 %copy-start = (bf16[352,1408]{1,0:T(8,128)(2,1)S(1)}, bf16[352,1408]{1,0:T(8,128)(2,1)}, u32[]{:S(2)}) copy-start(bf16[352,1408]{1,0:T(8,128)(2,1)} %param.20) | copy-start | bytes 2973700
  1.5 18.5 %all-to-all-start = ((s32[32,1,32]{2,1,0:T(1,128)}), s32[32,1,32]{2,1,0:T(1,128)S(1)}, u32[]{:S(2)}, u32[]{:S(2)}) async-start(s32[32,1,32]{2,1,0:T(1,128)} %broadcast_in_dim.64), calls=%async_computation | async-start | bytes 32768 | tf_op jit(solution)/shard_map/all_to_all | solution.py:129
  11.1 3.9 %copy-start.7 = (bf16[1408,352]{0,1:T(8,128)(2,1)S(1)}, bf16[1408,352]{0,1:T(8,128)(2,1)}, u32[]{:S(2)}) copy-start(bf16[1408,352]{0,1:T(8,128)(2,1)} %param.19) | copy-start | bytes 2973700
  15.0 1.2 copy-start.8
  16.9 2.8 copy-start.6
  20.0 20.0 %collective-permute-start = (bf16[2,512,352]{1,2,0:T(8,128)(2,1)S(1)}, bf16[2,512,352]{1,2,0:T(8,128)(2,1)}, u32[]{:S(2)}, u32[]{:S(2)}) collective-permute-start(bf16[2,512,352]{1,2,0:T(8,128)(2,1)S(1)} %pad_maximum_fusion), channel_id=1, source_target_pairs={{0,16},{4,20},{8,24},{12,28},{16,32},{20,36},{24,40},{28,44},{32,4... | collective-permute-start | bytes 2162696 | tf_op jit(solution)/shard_map/ppermute | solution.py:18
  25.6 29.8 %collective-permute-start.1 = (bf16[2,512,352]{1,2,0:T(8,128)(2,1)S(1)}, bf16[2,512,352]{1,2,0:T(8,128)(2,1)}, u32[]{:S(2)}, u32[]{:S(2)}) collective-permute-start(bf16[2,512,352]{1,2,0:T(8,128)(2,1)S(1)} %pad_maximum_fusion), channel_id=1, source_target_pairs={{0,12},{4,16},{8,20},{12,24},{16,28},{20,32},{24,36},{28,40},{32,4... | collective-permute-start | bytes 2162696 | tf_op jit(solution)/shard_map/ppermute | solution.py:18
  29.3 41.6 %collective-permute-start.2 = (bf16[2,512,352]{1,2,0:T(8,128)(2,1)S(1)}, bf16[2,512,352]{1,2,0:T(8,128)(2,1)}, u32[]{:S(2)}, u32[]{:S(2)}) collective-permute-start(bf16[2,512,352]{1,2,0:T(8,128)(2,1)S(1)} %pad_maximum_fusion), channel_id=1, source_target_pairs={{0,8},{4,12},{8,16},{12,20},{16,24},{20,28},{24,32},{28,36},{32,40... | collective-permute-start | bytes 2162696 | tf_op jit(solution)/shard_map/ppermute | solution.py:18
  32.4 47.0 %collective-permute-start.3 = (bf16[2,512,352]{1,2,0:T(8,128)(2,1)S(1)}, bf16[2,512,352]{1,2,0:T(8,128)(2,1)}, u32[]{:S(2)}, u32[]{:S(2)}) collective-permute-start(bf16[2,512,352]{1,2,0:T(8,128)(2,1)S(1)} %pad_maximum_fusion), channel_id=1, source_target_pairs={{0,4},{4,8},{8,12},{12,16},{16,20},{20,24},{24,28},{28,32},{32,36}... | collective-permute-start | bytes 2162696 | tf_op jit(solution)/shard_map/ppermute | solution.py:18
  34.3 46.3 %collective-permute-start.4 = (bf16[2,512,352]{1,2,0:T(8,128)(2,1)S(1)}, bf16[2,512,352]{1,2,0:T(8,128)(2,1)S(1)}, u32[]{:S(2)}, u32[]{:S(2)}) collective-permute-start(bf16[2,512,352]{1,2,0:T(8,128)(2,1)S(1)} %pad_maximum_fusion), channel_id=1, source_target_pairs={{4,0},{8,4},{12,8},{16,12},{20,16},{24,20},{28,24},{32,28},{36,32}... | collective-permute-start | bytes 2162696 | tf_op jit(solution)/shard_map/ppermute | solution.py:18
  40.0 40.7 %collective-permute-start.5 = (bf16[2,512,352]{1,2,0:T(8,128)(2,1)S(1)}, bf16[2,512,352]{1,2,0:T(8,128)(2,1)S(1)}, u32[]{:S(2)}, u32[]{:S(2)}) collective-permute-start(bf16[2,512,352]{1,2,0:T(8,128)(2,1)S(1)} %pad_maximum_fusion), channel_id=1, source_target_pairs={{8,0},{12,4},{16,8},{20,12},{24,16},{28,20},{32,24},{36,28},{40,32... | collective-permute-start | bytes 2162696 | tf_op jit(solution)/shard_map/ppermute | solution.py:18
  55.4 34.1 %collective-permute-start.6 = (bf16[2,512,352]{1,2,0:T(8,128)(2,1)S(1)}, bf16[2,512,352]{1,2,0:T(8,128)(2,1)S(1)}, u32[]{:S(2)}, u32[]{:S(2)}) collective-permute-start(bf16[2,512,352]{1,2,0:T(8,128)(2,1)S(1)} %pad_maximum_fusion), channel_id=1, source_target_pairs={{12,0},{16,4},{20,8},{24,12},{28,16},{32,20},{36,24},{40,28},{44,3... | collective-permute-start | bytes 2162696 | tf_op jit(solution)/shard_map/ppermute | solution.py:18
  70.9 32.8 %collective-permute-start.7 = (bf16[2,512,352]{1,2,0:T(8,128)(2,1)S(1)}, bf16[2,512,352]{1,2,0:T(8,128)(2,1)S(1)}, u32[]{:S(2)}, u32[]{:S(2)}) collective-permute-start(bf16[2,512,352]{1,2,0:T(8,128)(2,1)S(1)} %pad_maximum_fusion), channel_id=1, source_target_pairs={{16,0},{20,4},{24,8},{28,12},{32,16},{36,20},{40,24},{44,28},{48,3... | collective-permute-start | bytes 2162696 | tf_op jit(solution)/shard_map/ppermute | solution.py:18
  103.7 3.2 %copy-start.10 = (bf16[512,352]{0,1:T(8,128)(2,1)S(1)}, bf16[512,352]{0,1:T(8,128)(2,1)}, u32[]{:S(2)}) copy-start(bf16[512,352]{0,1:T(8,128)(2,1)} %convolution_convert_fusion.2) | copy-start | bytes 1081348
  125.2 17.5 %copy-start.3 = (bf16[1,4608,352]{1,2,0:T(8,128)(2,1)S(1)}, bf16[1,4608,352]{1,2,0:T(8,128)(2,1)}, u32[]{:S(2)}) copy-start(bf16[1,4608,352]{1,2,0:T(8,128)(2,1)} %get-tuple-element.20) | copy-start | bytes 9732100
  157.9 6.5 %copy-start.2 = (bf16[512,1408]{1,0:T(8,128)(2,1)S(1)}, bf16[512,1408]{1,0:T(8,128)(2,1)}, u32[]{:S(2)}) copy-start(bf16[512,1408]{1,0:T(8,128)(2,1)} %param.13) | copy-start | bytes 4325380
  160.1 22.6 %all-to-all-start.1 = ((bf16[4,128,1408]{2,1,0:T(8,128)(2,1)}), bf16[4,128,1408]{2,1,0:T(8,128)(2,1)}, u32[]{:S(2)}, u32[]{:S(2)}) async-start(bf16[4,128,1408]{2,1,0:T(8,128)(2,1)} %bitcast.53), calls=%async_computation.1 | async-start | bytes 2883584 | tf_op jit(solution)/shard_map/all_to_all | solution.py:37
  166.2 19.4 %copy-start.4 = (f32[1408]{0:T(1024)S(1)}, f32[1408]{0:T(1024)}, u32[]{:S(2)}) copy-start(f32[1408]{0:T(1024)} %param.21) | copy-start | bytes 16900
  205.3 18.4 %copy-start.9 = (s32[32]{0:T(128)S(1)}, s32[32]{0:T(128)}, u32[]{:S(2)}) copy-start(s32[32]{0:T(128)} %param.15) | copy-start | bytes 388
  220.0 20.1 %copy-start.5 = (f32[1408]{0:T(1024)S(1)}, f32[1408]{0:T(1024)}, u32[]{:S(2)}) copy-start(f32[1408]{0:T(1024)} %param.24) | copy-start | bytes 16900
  220.0 19.7 %all-to-all-start.3 = ((bf16[4,128,1408]{2,1,0:T(8,128)(2,1)}), bf16[4,128,1408]{2,1,0:T(8,128)(2,1)S(1)}, u32[]{:S(2)}, u32[]{:S(2)}) async-start(bf16[4,128,1408]{2,1,0:T(8,128)(2,1)} %bitcast.57), calls=%async_computation.3 | async-start | bytes 2883584 | tf_op jit(solution)/shard_map/all_to_all | solution.py:37
  241.5 19.2 %all-to-all-start.4 = ((bf16[4,128,1408]{2,1,0:T(8,128)(2,1)}), bf16[4,128,1408]{2,1,0:T(8,128)(2,1)}, u32[]{:S(2)}, u32[]{:S(2)}) async-start(bf16[4,128,1408]{2,1,0:T(8,128)(2,1)} %broadcast_in_dim.126), calls=%async_computation.4 | async-start | bytes 2883584 | tf_op jit(solution)/shard_map/all_to_all | solution.py:44
  269.7 17.7 %all-to-all-start.5 = ((bf16[32,4,896]{2,1,0:T(4,128)(2,1)}), bf16[32,4,896]{2,1,0:T(4,128)(2,1)S(1)}, u32[]{:S(2)}, u32[]{:S(2)}) async-start(bf16[32,4,896]{2,1,0:T(4,128)(2,1)} %bitcast.51), calls=%async_computation.5 | async-start | bytes 458752 | tf_op jit(solution)/shard_map/all_to_all | solution.py:76
  290.7 19.7 %all-to-all-start.6 = ((bf16[32,16,896]{2,1,0:T(8,128)(2,1)}), bf16[32,16,896]{2,1,0:T(8,128)(2,1)S(1)}, u32[]{:S(2)}, u32[]{:S(2)}) async-start(bf16[32,16,896]{2,1,0:T(8,128)(2,1)} %select_select_fusion), calls=%async_computation.6 | async-start | bytes 1835008 | tf_op jit(solution)/shard_map/all_to_all | solution.py:96
  294.5 17.8 %copy-start.1 = (bf16[352,1408]{1,0:T(8,128)(2,1)S(1)}, bf16[352,1408]{1,0:T(8,128)(2,1)}, u32[]{:S(2)}) copy-start(bf16[352,1408]{1,0:T(8,128)(2,1)} %param.20) | copy-start | bytes 2973700
